TPU v7x, 128 devices: a whole 4x4x4 slice. The times are simulated.
128 devices in a mesh: date: 16 (over z, x), space: 8 (over y, core).
Axes of the slice: x: 4, y: 4, z: 4, core: 2. Of those that a mesh axis runs over, the one named last changes fastest.
Arguments:
- frames: bfloat16 [64, 2048, 1024], P('date', 'space'), may hold values from -6 to 6
- cloud_mask: int32 [64, 2048], P('date', 'space'), may hold values from 0 to 1
- qkv_weight: bfloat16 [2, 1024, 3072], replicated, may hold values from -0.1875 to 0.1875
- out_weight: bfloat16 [2, 1024, 1024], replicated, may hold values from -0.1875 to 0.1875
- norm_gain: float32 [2, 1024], replicated, may hold values from 0.1 to 1.9
- head_norm_scale: float32 [2, 1024], replicated, may hold values from 0.1 to 1.9
- decay: float32 [2, 64, 16], P(None, 'date'), as said below
Outputs:
- forecast: bfloat16 [64, 2048, 1024], P('date', 'space')
Inputs may be any that keep to these rules, and one draw needn't show every extreme that they name: `decay`: every entry lies strictly between 0 and 1.
All inputs are finite; a program needn't handle non-finite values.
Results may differ from a plain program's by a relative error of at most 0.0065.
Values may be sent and summed in bfloat16 or wider, within the bound.
No kernel may reach another device: no remote copies, remote signals or barrier semaphores. Data moves between devices by JAX's collectives and lax.ppermute only.
A program may use at most 128 MiB of HBM per device.

v0:
```python
import jax
import jax.numpy as jnp
from jax import lax
from jax.experimental import pallas as pl
from jax.experimental.pallas import tpu as pltpu
from jax.sharding import PartitionSpec as P

HEADS = 16
HEAD = 64
STACK_LEVELS = 2


def feature(u):
    return jax.nn.elu(u) + 1.0


def kv_chunks(normed, flags, weights, layer, n_dev):
    dates, tokens, width = normed.shape
    per_head = n_dev // HEADS
    rows = HEAD // per_head
    block = 4 * HEAD

    def body(x_ref, m_ref, wk_ref, wv_ref, o_ref):
        t = pl.program_id(0)
        x = x_ref[0]
        u = jnp.dot(x, wk_ref[0], preferred_element_type=jnp.float32)
        key = jnp.where(u > 0, u + 1.0, jnp.exp(jnp.minimum(u, 0.0))) * m_ref[0]
        key = key.astype(jnp.bfloat16)
        value = jnp.dot(x, wv_ref[0], preferred_element_type=jnp.float32).astype(jnp.bfloat16)
        blocks = [
            lax.dot_general(
                key[:, b * block : (b + 1) * block],
                value[:, b * block : (b + 1) * block],
                (((0,), (0,)), ((), ())),
                preferred_element_type=jnp.float32,
            )
            for b in range(width // block)
        ]
        for date in range(dates):

            @pl.when(t == date)
            def _():
                for b, kv in enumerate(blocks):
                    for i in range(block // HEAD):
                        h = b * (block // HEAD) + i
                        for rb in range(per_head):
                            o_ref[h * per_head + rb, :, date * HEAD : (date + 1) * HEAD] = kv[
                                i * HEAD + rb * rows : i * HEAD + (rb + 1) * rows,
                                i * HEAD : (i + 1) * HEAD,
                            ]

    return pl.pallas_call(
        body,
        grid=(dates,),
        out_shape=jax.ShapeDtypeStruct((n_dev, rows, dates * HEAD), jnp.float32),
        in_specs=[
            pl.BlockSpec((1, tokens, width), lambda t: (t, 0, 0)),
            pl.BlockSpec((1, tokens, 1), lambda t: (t, 0, 0)),
            pl.BlockSpec((1, width, width), lambda t: (layer, 0, 1)),
            pl.BlockSpec((1, width, width), lambda t: (layer, 0, 2)),
        ],
        out_specs=pl.BlockSpec((n_dev, rows, dates * HEAD), lambda t: (0, 0, 0)),
        compiler_params=pltpu.CompilerParams(dimension_semantics=("arbitrary",)),
    )(normed, flags, weights, weights)


def shards(frames, cloud_mask, qkv_weight, out_weight, norm_gain, head_norm_scale, decay):
    dates_here, tokens_here, width = frames.shape
    heads = HEADS
    n_space = lax.axis_size("space")
    n_date = lax.axis_size("date")
    n_dev = n_date * n_space
    everyone = ("date", "space")
    me = lax.axis_index("date") * n_space + lax.axis_index("space")
    entries = heads * HEAD * HEAD // n_dev
    per_head = n_dev // heads
    dates_all = n_date * dates_here
    to_each = jnp.repeat(jnp.transpose(decay, (2, 0, 1)), per_head, axis=0)
    from_each = lax.all_to_all(to_each, everyone, 0, 0, tiled=True)
    my_decay = from_each.reshape(n_date, n_space, STACK_LEVELS, dates_here)[:, 0]
    my_decay = jnp.transpose(my_decay, (1, 0, 2)).reshape(STACK_LEVELS, dates_all)
    pos = jnp.arange(dates_all)
    current = frames
    flag_f = cloud_mask.astype(jnp.float32)[:, :, None]
    for layer in range(STACK_LEVELS):
        xf = current.astype(jnp.float32)
        in_msq = jnp.mean(xf * xf, -1, keepdims=True) + 1e-05
        normalized_output = (xf * lax.rsqrt(in_msq) * norm_gain[layer]).astype(jnp.bfloat16)
        flat = normalized_output.reshape(-1, width)
        pieces = lax.all_to_all(
            kv_chunks(normalized_output, flag_f, qkv_weight, layer, n_dev), everyone, 0, 0, tiled=True
        )
        rows = pieces.shape[1]
        kv = pieces.reshape(n_date, n_space, rows, dates_here, HEAD).sum(1)
        kv = jnp.transpose(kv, (0, 2, 1, 3)).reshape(dates_all, entries)
        d = my_decay[layer]
        inside = (pos[None, None, :] > pos[None, :, None]) & (pos[None, None, :] <= pos[:, None, None])
        weight = jnp.prod(jnp.where(inside, d[None, None, :], 1.0), axis=2)
        weight = jnp.where(pos[None, :] <= pos[:, None], weight, 0.0)
        states = jnp.dot(weight, kv, precision=lax.Precision.HIGHEST, preferred_element_type=jnp.float32)
        proj_q = jnp.dot(flat, qkv_weight[layer, :, :width], preferred_element_type=jnp.float32)
        query = (
            feature(proj_q)
            .astype(jnp.bfloat16)
            .reshape(dates_here, tokens_here, heads, HEAD)
        )
        states, query = lax.optimization_barrier((states, query))
        state_b = states.astype(jnp.bfloat16).reshape(n_date, 1, dates_here, entries)
        outgoing = jnp.broadcast_to(state_b, (n_date, n_space, dates_here, entries)).reshape(
            n_dev, dates_here, entries
        )
        back = lax.all_to_all(outgoing, everyone, 0, 0, tiled=True)
        state_b = jnp.transpose(back, (1, 0, 2)).reshape(dates_here, heads, HEAD, HEAD)

        numer = jnp.einsum("tshe,thef->tshf", query, state_b, preferred_element_type=jnp.float32)
        head_msq = jnp.mean(numer * numer, -1, keepdims=True) + 1e-05
        numer = numer * lax.rsqrt(head_msq)
        mixed = (numer.reshape(dates_here, tokens_here, width) * head_norm_scale[layer]).astype(
            jnp.bfloat16
        )
        update = jnp.dot(
            mixed.reshape(-1, width), out_weight[layer], preferred_element_type=jnp.float32
        )
        current = (xf + update.reshape(dates_here, tokens_here, width)).astype(jnp.bfloat16)
    return current


def solution(mesh):
    placed = (
        P("date", "space", None),
        P("date", "space"),
        P(),
        P(),
        P(),
        P(),
        P(None, "date", None),
    )
    return jax.shard_map(
        shards, mesh=mesh, in_specs=placed, out_specs=P("date", "space", None), check_vma=False
    )
```

profile of v0, /device:TPU:1, one launch (start us, length us, event | category | flops | bytes accessed | tf_op | source)
XLA Modules:
  0.0 164.9 jit_solution(12739182364004776190)
XLA Ops:
  1.6 11.5 %all-to-all-start = ((f32[128,2,4]{2,1,0:T(2,128)}), f32[128,2,4]{2,1,0:T(2,128)S(1)}, u32[]{:S(2)}, u32[]{:S(2)}) async-start(f32[128,2,4]{2,1,0:T(2,128)} %bitcast.1), calls=%async_computation | async-start | bytes 262144 | tf_op jit(solution)/shard_map/all_to_all | solution.py:79
  13.9 2.1 %fusion = f32[4,256]{1,0:T(4,128)S(1)} fusion(bf16[4,256,1024]{2,1,0:T(8,128)(2,1)} %param.7), kind=kLoop, calls=%fused_computation.10 | loop fusion | flops 3144704 | bytes 2101248 | tf_op jit(solution)/shard_map/reduce_sum | solution.py:87
  16.0 1.9 %fusion.2.x_ref = bf16[4,256,1024]{2,1,0:T(8,128)(2,1)} fusion(bf16[4,256,1024]{2,1,0:T(8,128)(2,1)S(1)} %copy-done.2, f32[1024]{0:T(1024)S(1)} %bitcast.89, f32[4,256]{1,0:T(4,128)S(1)} %add_rsqrt_fusion.3), kind=kLoop, calls=%fused_computation.12 | loop fusion | flops 4194304 | bytes 4202496 | tf_op jit(solution)/shard_map/convert_element_type | solution.py:88
  18.9 10.4 %shard_map.73 = f32[128,8,256]{2,1,0:T(8,128)} custom-call(bf16[4,256,1024]{2,1,0:T(8,128)(2,1)} %fusion.2.x_ref, f32[4,256,1]{2,1,0:T(8,128)} %copy.64.m_ref, bf16[2,1024,3072]{2,1,0:T(8,128)(2,1)} %wv_ref.3, bf16[2,1024,3072]{2,1,0:T(8,128)(2,1)} %wv_ref.3), custom_call_target="tpu_custom_call" | custom-call | tf_op jit(solution)/shard_map/pallas_call | solution.py:52
  29.3 9.8 %all-to-all-start.1 = ((f32[128,8,256]{2,1,0:T(8,128)}), f32[128,8,256]{2,1,0:T(8,128)S(1)}, u32[]{:S(2)}, u32[]{:S(2)}) async-start(f32[128,8,256]{2,1,0:T(8,128)} %shard_map.73), calls=%async_computation.1 | async-start | bytes 2097152 | tf_op jit(solution)/shard_map/all_to_all | solution.py:90
  39.1 6.3 %fusion.10 = bf16[1024,1024]{1,0:T(8,128)(2,1)} fusion(bf16[1024,1024]{1,0:T(8,128)(2,1)S(1)} %bitcast.78, bf16[2,1024,3072]{2,1,0:T(8,128)(2,1)} %wv_ref.3), kind=kOutput, calls=%fused_computation.20 | convolution fusion | flops 2152726528 | bytes 6291456 | tf_op jit(solution)/shard_map/dot_general | solution.py:101
  45.4 4.0 %copy.66 = bf16[1024,1024]{0,1:T(8,128)(2,1)} copy(bf16[1024,1024]{1,0:T(8,128)(2,1)} %fusion.10) | data formatting | bytes 4194304 | tf_op jit(solution)/shard_map/convert_element_type | solution.py:104
  49.4 3.3 %reshape.159 = bf16[4,256,16,64]{1,0,3,2:T(4,128)(2,1)S(1)} reshape(bf16[1024,1024]{0,1:T(8,128)(2,1)} %copy.66) | data formatting | bytes 4194304 | tf_op jit(solution)/shard_map/reshape | solution.py:105
  53.2 2.2 %fusion.21 = (f32[64,64]{1,0:T(8,128)S(1)}, f32[64,64]{1,0:T(8,128)S(1)}) fusion(f32[64]{0:T(128)S(1)} %broadcast_in_dim.75, pred[64,64]{1,0:T(8,128)(4,1)S(1)} %get-tuple-element.28, pred[64,64]{1,0:T(8,128)(4,1)S(1)} %get-tuple-element.27, f32[64]{0:T(128)S(1)} %broadcast_in_dim.68), kind=kLoop, calls=%fused_computation.37 | loop fusion | flops 1302528 | bytes 41472 | tf_op jit(solution)/shard_map/reduce_prod | solution.py:98
  55.4 2.4 %all-to-all-done.1 = f32[128,8,256]{2,1,0:T(8,128)S(1)} async-done(((f32[128,8,256]{2,1,0:T(8,128)}), f32[128,8,256]{2,1,0:T(8,128)S(1)}, u32[]{:S(2)}, u32[]{:S(2)}) %all-to-all-start.1) | async-done | bytes 1048608 | tf_op jit(solution)/shard_map/all_to_all | solution.py:90
  57.8 2.2 %reshape.156 = f32[16,8,8,4,64]{4,3,2,1,0:T(4,128)} reshape(f32[128,8,256]{2,1,0:T(8,128)S(1)} %all-to-all-done.1) | data formatting | bytes 2097152 | tf_op jit(solution)/shard_map/reshape | solution.py:94
  60.1 2.2 %reduce_sum.55 = f32[16,8,4,64]{3,2,1,0:T(4,128)S(1)} reduce(f32[16,8,8,4,64]{4,3,2,1,0:T(4,128)} %reshape.156, f32[]{:T(128)} %constant.18.clone.1), dimensions={1}, to_apply=%region_2.3 | reduce | flops 229376 | bytes 1179652 | tf_op jit(solution)/shard_map/reduce_sum | solution.py:94
  63.6 7.4 %all-to-all-start.2 = ((bf16[128,4,512]{2,1,0:T(4,128)(2,1)}), bf16[128,4,512]{2,1,0:T(4,128)(2,1)S(1)}, u32[]{:S(2)}, u32[]{:S(2)}) async-start(bf16[128,4,512]{2,1,0:T(4,128)(2,1)} %bitcast.9), calls=%async_computation.2 | async-start | bytes 1048576 | tf_op jit(solution)/shard_map/all_to_all | solution.py:112
  71.1 13.4 %all-to-all-done.2 = bf16[128,4,512]{2,1,0:T(4,128)(2,1)S(1)} async-done(((bf16[128,4,512]{2,1,0:T(4,128)(2,1)}), bf16[128,4,512]{2,1,0:T(4,128)(2,1)S(1)}, u32[]{:S(2)}, u32[]{:S(2)}) %all-to-all-start.2) | async-done | bytes 524320 | tf_op jit(solution)/shard_map/all_to_all | solution.py:112
  85.4 1.6 reshape.161
  89.6 1.2 copy-done.8
  90.9 2.7 %fusion.4 = (f32[4,256]{1,0:T(4,128)S(1)}, bf16[4,256,1024]{2,1,0:T(8,128)(2,1)S(1)}) fusion(bf16[4,256,1024]{1,2,0:T(8,128)(2,1)S(1)} %bitcast.80, bf16[2,1024,1024]{2,1,0:T(8,128)(2,1)S(1)} %copy-done.8, bf16[4,256,1024]{2,1,0:T(8,128)(2,1)S(1)} %copy-done.3), kind=kOutput, calls=%fused_computation.14 | convolution fusion | flops 2153774080 | bytes 8392704 | tf_op jit(solution)/shard_map/dot_general | solution.py:121
  93.6 1.3 copy-done.4
  94.9 1.9 %fusion.6.x_ref = bf16[4,256,1024]{2,1,0:T(8,128)(2,1)} fusion(bf16[4,256,1024]{2,1,0:T(8,128)(2,1)S(1)} %get-tuple-element.24, f32[1024]{0:T(1024)S(1)} %bitcast.88, f32[4,256]{1,0:T(4,128)S(1)} %add_rsqrt_fusion.2), kind=kLoop, calls=%fused_computation.16 | loop fusion | flops 4194304 | bytes 4202496 | tf_op jit(solution)/shard_map/convert_element_type | solution.py:88
  96.8 10.4 %shard_map.74 = f32[128,8,256]{2,1,0:T(8,128)} custom-call(bf16[4,256,1024]{2,1,0:T(8,128)(2,1)} %fusion.6.x_ref, f32[4,256,1]{2,1,0:T(8,128)} %copy.64.m_ref, bf16[2,1024,3072]{2,1,0:T(8,128)(2,1)} %wv_ref.3, bf16[2,1024,3072]{2,1,0:T(8,128)(2,1)} %wv_ref.3), custom_call_target="tpu_custom_call" | custom-call | tf_op jit(solution)/shard_map/pallas_call | solution.py:52
  107.2 4.6 %all-to-all-start.3 = ((f32[128,8,256]{2,1,0:T(8,128)}), f32[128,8,256]{2,1,0:T(8,128)S(1)}, u32[]{:S(2)}, u32[]{:S(2)}) async-start(f32[128,8,256]{2,1,0:T(8,128)} %shard_map.74), calls=%async_computation.3 | async-start | bytes 2097152 | tf_op jit(solution)/shard_map/all_to_all | solution.py:90
  111.8 6.4 %fusion.13 = bf16[1024,1024]{1,0:T(8,128)(2,1)} fusion(bf16[1024,1024]{1,0:T(8,128)(2,1)S(1)} %bitcast.79, bf16[2,1024,3072]{2,1,0:T(8,128)(2,1)} %wv_ref.3), kind=kOutput, calls=%fused_computation.23 | convolution fusion | flops 2152726528 | bytes 6291456 | tf_op jit(solution)/shard_map/dot_general | solution.py:101
  118.1 4.0 %copy.74 = bf16[1024,1024]{0,1:T(8,128)(2,1)} copy(bf16[1024,1024]{1,0:T(8,128)(2,1)} %fusion.13) | data formatting | bytes 4194304 | tf_op jit(solution)/shard_map/convert_element_type | solution.py:104
  122.1 3.3 %reshape.165 = bf16[4,256,16,64]{1,0,3,2:T(4,128)(2,1)S(1)} reshape(bf16[1024,1024]{0,1:T(8,128)(2,1)} %copy.74) | data formatting | bytes 4194304 | tf_op jit(solution)/shard_map/reshape | solution.py:105
  125.4 5.2 %all-to-all-done.3 = f32[128,8,256]{2,1,0:T(8,128)S(1)} async-done(((f32[128,8,256]{2,1,0:T(8,128)}), f32[128,8,256]{2,1,0:T(8,128)S(1)}, u32[]{:S(2)}, u32[]{:S(2)}) %all-to-all-start.3) | async-done | bytes 1048608 | tf_op jit(solution)/shard_map/all_to_all | solution.py:90
  130.7 2.2 %reshape.162 = f32[16,8,8,4,64]{4,3,2,1,0:T(4,128)} reshape(f32[128,8,256]{2,1,0:T(8,128)S(1)} %all-to-all-done.3) | data formatting | bytes 2097152 | tf_op jit(solution)/shard_map/reshape | solution.py:94
  132.9 2.2 %reduce_sum.58 = f32[16,8,4,64]{3,2,1,0:T(4,128)S(1)} reduce(f32[16,8,8,4,64]{4,3,2,1,0:T(4,128)} %reshape.162, f32[]{:T(128)} %constant.18.clone.1), dimensions={1}, to_apply=%region_6.7 | reduce | flops 229376 | bytes 1179652 | tf_op jit(solution)/shard_map/reduce_sum | solution.py:94
  136.5 4.8 %all-to-all-start.4 = ((bf16[128,4,512]{2,1,0:T(4,128)(2,1)}), bf16[128,4,512]{2,1,0:T(4,128)(2,1)S(1)}, u32[]{:S(2)}, u32[]{:S(2)}) async-start(bf16[128,4,512]{2,1,0:T(4,128)(2,1)} %bitcast.19), calls=%async_computation.4 | async-start | bytes 1048576 | tf_op jit(solution)/shard_map/all_to_all | solution.py:112
  141.3 13.6 %all-to-all-done.4 = bf16[128,4,512]{2,1,0:T(4,128)(2,1)S(1)} async-done(((bf16[128,4,512]{2,1,0:T(4,128)(2,1)}), bf16[128,4,512]{2,1,0:T(4,128)(2,1)S(1)}, u32[]{:S(2)}, u32[]{:S(2)}) %all-to-all-start.4) | async-done | bytes 524320 | tf_op jit(solution)/shard_map/all_to_all | solution.py:112
  155.8 1.6 reshape.167
  160.0 1.2 copy-done.9
  161.2 3.7 %fusion.7 = bf16[4,256,1024]{2,1,0:T(8,128)(2,1)} fusion(bf16[4,256,1024]{2,1,0:T(8,128)(2,1)S(1)} %copy-done.5, bf16[4,256,1024]{1,2,0:T(8,128)(2,1)S(1)} %bitcast.81, bf16[2,1024,1024]{2,1,0:T(8,128)(2,1)S(1)} %copy-done.9), kind=kOutput, calls=%fused_computation.17 | convolution fusion | flops 2150629376 | bytes 8388608 | tf_op jit(solution)/shard_map/dot_general | solution.py:121
  (54 shorter events, 13.5 us)
Async XLA Ops:
  0.0 16.0 %copy-start.2 = (bf16[4,256,1024]{2,1,0:T(8,128)(2,1)S(1)}, bf16[4,256,1024]{2,1,0:T(8,128)(2,1)}, u32[]{:S(2)}) copy-start(bf16[4,256,1024]{2,1,0:T(8,128)(2,1)} %param.7) | copy-start | bytes 6291460
  1.6 27.7 %all-to-all-start = ((f32[128,2,4]{2,1,0:T(2,128)}), f32[128,2,4]{2,1,0:T(2,128)S(1)}, u32[]{:S(2)}, u32[]{:S(2)}) async-start(f32[128,2,4]{2,1,0:T(2,128)} %bitcast.1), calls=%async_computation | async-start | bytes 262144 | tf_op jit(solution)/shard_map/all_to_all | solution.py:79
  16.0 1.9 %copy-start.7 = (s32[4,256]{1,0:T(4,128)S(1)}, s32[4,256]{1,0:T(4,128)}, u32[]{:S(2)}) copy-start(s32[4,256]{1,0:T(4,128)} %param.8) | copy-start | bytes 12292
  29.3 9.8 %copy-start = (bf16[4,256,1024]{2,1,0:T(8,128)(2,1)S(1)}, bf16[4,256,1024]{2,1,0:T(8,128)(2,1)}, u32[]{:S(2)}) copy-start(bf16[4,256,1024]{2,1,0:T(8,128)(2,1)} %fusion.2.x_ref) | copy-start | bytes 6291460
  29.3 28.6 %all-to-all-start.1 = ((f32[128,8,256]{2,1,0:T(8,128)}), f32[128,8,256]{2,1,0:T(8,128)S(1)}, u32[]{:S(2)}, u32[]{:S(2)}) async-start(f32[128,8,256]{2,1,0:T(8,128)} %shard_map.73), calls=%async_computation.1 | async-start | bytes 2097152 | tf_op jit(solution)/shard_map/all_to_all | solution.py:90
  60.1 11.0 %copy-start.6 = (f32[2,1024]{1,0:T(2,128)S(1)}, f32[2,1024]{1,0:T(2,128)}, u32[]{:S(2)}) copy-start(f32[2,1024]{1,0:T(2,128)} %param.12) | copy-start | bytes 24580
  63.6 20.9 %all-to-all-start.2 = ((bf16[128,4,512]{2,1,0:T(4,128)(2,1)}), bf16[128,4,512]{2,1,0:T(4,128)(2,1)S(1)}, u32[]{:S(2)}, u32[]{:S(2)}) async-start(bf16[128,4,512]{2,1,0:T(4,128)(2,1)} %bitcast.9), calls=%async_computation.2 | async-start | bytes 1048576 | tf_op jit(solution)/shard_map/all_to_all | solution.py:112
  88.0 1.6 copy-start.3
  88.0 2.8 %copy-start.8 = (bf16[2,1024,1024]{2,1,0:T(8,128)(2,1)S(1)}, bf16[2,1024,1024]{2,1,0:T(8,128)(2,1)}, u32[]{:S(2)}) copy-start(bf16[2,1024,1024]{2,1,0:T(8,128)(2,1)} %param.10) | copy-start | bytes 12582916
  93.6 1.3 copy-start.4
  107.2 4.6 %copy-start.1 = (bf16[4,256,1024]{2,1,0:T(8,128)(2,1)S(1)}, bf16[4,256,1024]{2,1,0:T(8,128)(2,1)}, u32[]{:S(2)}) copy-start(bf16[4,256,1024]{2,1,0:T(8,128)(2,1)} %fusion.6.x_ref) | copy-start | bytes 6291460
  107.2 23.5 %all-to-all-start.3 = ((f32[128,8,256]{2,1,0:T(8,128)}), f32[128,8,256]{2,1,0:T(8,128)S(1)}, u32[]{:S(2)}, u32[]{:S(2)}) async-start(f32[128,8,256]{2,1,0:T(8,128)} %shard_map.74), calls=%async_computation.3 | async-start | bytes 2097152 | tf_op jit(solution)/shard_map/all_to_all | solution.py:90
  136.5 18.5 %all-to-all-start.4 = ((bf16[128,4,512]{2,1,0:T(4,128)(2,1)}), bf16[128,4,512]{2,1,0:T(4,128)(2,1)S(1)}, u32[]{:S(2)}, u32[]{:S(2)}) async-start(bf16[128,4,512]{2,1,0:T(4,128)(2,1)} %bitcast.19), calls=%async_computation.4 | async-start | bytes 1048576 | tf_op jit(solution)/shard_map/all_to_all | solution.py:112
  158.4 1.6 copy-start.5
  158.4 2.8 %copy-start.9 = (bf16[2,1024,1024]{2,1,0:T(8,128)(2,1)S(1)}, bf16[2,1024,1024]{2,1,0:T(8,128)(2,1)}, u32[]{:S(2)}) copy-start(bf16[2,1024,1024]{2,1,0:T(8,128)(2,1)} %param.10) | copy-start | bytes 12582916
where the time goes:
time: 166 us; the launch traced here: 165 us
  starting transfers between devices  38 us (23%)
  local copies, waits for them, and re-layouts  36.2 us (22%)
  waiting for transfers between devices  34.7 us (21%)
  matrix products  21.4 us (13%)
  Pallas kernels  20.8 us (13%)
  other arithmetic  13.6 us (8%)
    all_to_all x2, waiting for transfers between devices, shards(): back = lax.all_to_all(outgoing, everyone, 0, 0, tiled=True)  27.1 us
    pallas_call x2, Pallas kernels, kv_chunks(): pl.pallas_call(body, grid=(dates,), out_shape=jax.ShapeDtypeStruct((n_dev...  20.8 us
    all_to_all x2, starting transfers between devices, shards(): lax.all_to_all(kv_chunks(normalized_output, flag_f, qkv_weight, layer, n_...  14.3 us
    dot_general x2, matrix products, shards(): jnp.dot(flat, qkv_weight[layer, :, :width], preferred_element_type=jnp.fl...  12.7 us
    all_to_all x2, starting transfers between devices, shards(): back = lax.all_to_all(outgoing, everyone, 0, 0, tiled=True)  12.1 us
    all_to_all x1, starting transfers between devices, shards(): from_each = lax.all_to_all(to_each, everyone, 0, 0, tiled=True)  11.5 us
    convert_element_type x2, local copies, waits for them, and re-layouts, shards(): query = feature(proj_q).astype(jnp.bfloat16).reshape(dates_here, tokens_h...  7.9 us
    all_to_all x2, waiting for transfers between devices, shards(): lax.all_to_all(kv_chunks(normalized_output, flag_f, qkv_weight, layer, n_...  7.65 us
  transfers between devices with their start and end apart: 5, of which 4 were waited for; matrix products, arithmetic and copies ran while one was open for 22% of the time, Pallas kernels for 6%

commit v1 on v0

--- a/solution.py
+++ b/solution.py
@@ -91,7 +91,8 @@
             kv_chunks(normalized_output, flag_f, qkv_weight, layer, n_dev), everyone, 0, 0, tiled=True
         )
         rows = pieces.shape[1]
-        kv = pieces.reshape(n_date, n_space, rows, dates_here, HEAD).sum(1)
+        kv = pieces.reshape(n_date, n_space, rows, dates_here * HEAD).sum(1)
+        kv = lax.optimization_barrier(kv).reshape(n_date, rows, dates_here, HEAD)
         kv = jnp.transpose(kv, (0, 2, 1, 3)).reshape(dates_all, entries)
         d = my_decay[layer]
         inside = (pos[None, None, :] > pos[None, :, None]) & (pos[None, None, :] <= pos[:, None, None])

time: 166 us -> 159 us (0.958)
  local copies, waits for them, and re-layouts: 36.2 us -> 31.8 us
  other arithmetic: 13.6 us -> 10.9 us
    reduce_sum x2, other arithmetic: 4.42 us -> 0.13 us  [shards(): kv = pieces.reshape(n_date, n_space, rows, dates_here * HEAD).sum(1)]
    reshape x2, local copies, waits for them, and re-layouts: 4.45 us -> 0.31 us  [shards(): kv = lax.optimization_barrier(kv).reshape(n_date, rows, dates_here, HEAD)]
    unnamed x22 -> x20, local copies, waits for them, and re-layouts: 6.93 us -> 6.73 us
  transfers between devices with their start and end apart: 5 -> 5, of which waited for: 4 -> 4; matrix products, arithmetic and copies ran while one was open for 22% -> 24% of each run, Pallas kernels for 6% -> 7%
where the time goes in v1:
time: 159 us; the launch traced here: 158 us
  starting transfers between devices  38.1 us (24%)
  waiting for transfers between devices  34.6 us (22%)
  local copies, waits for them, and re-layouts  31.8 us (20%)
  matrix products  21.4 us (13%)
  Pallas kernels  21 us (13%)
  other arithmetic  10.9 us (7%)
    all_to_all x2, waiting for transfers between devices, shards(): back = lax.all_to_all(outgoing, everyone, 0, 0, tiled=True)  27.1 us
    pallas_call x2, Pallas kernels, kv_chunks(): pl.pallas_call(body, grid=(dates,), out_shape=jax.ShapeDtypeStruct((n_dev...  21 us
    all_to_all x2, starting transfers between devices, shards(): lax.all_to_all(kv_chunks(normalized_output, flag_f, qkv_weight, layer, n_...  14.3 us
    dot_general x2, matrix products, shards(): jnp.dot(flat, qkv_weight[layer, :, :width], preferred_element_type=jnp.fl...  12.7 us
    all_to_all x2, starting transfers between devices, shards(): back = lax.all_to_all(outgoing, everyone, 0, 0, tiled=True)  12.4 us
    all_to_all x1, starting transfers between devices, shards(): from_each = lax.all_to_all(to_each, everyone, 0, 0, tiled=True)  11.5 us
    convert_element_type x2, local copies, waits for them, and re-layouts, shards(): query = feature(proj_q).astype(jnp.bfloat16).reshape(dates_here, tokens_h...  7.9 us
    all_to_all x2, waiting for transfers between devices, shards(): lax.all_to_all(kv_chunks(normalized_output, flag_f, qkv_weight, layer, n_...  7.56 us
  transfers between devices with their start and end apart: 5, of which 4 were waited for; matrix products, arithmetic and copies ran while one was open for 24% of the time, Pallas kernels for 7%

profile of v1, /device:TPU:1, one launch (start us, length us, event | category | flops | bytes accessed | tf_op | source)
XLA Modules:
  0.0 158.3 jit_solution(7918966668124419225)
XLA Ops:
  1.5 11.5 %all-to-all-start = ((f32[128,2,4]{2,1,0:T(2,128)}), f32[128,2,4]{2,1,0:T(2,128)S(1)}, u32[]{:S(2)}, u32[]{:S(2)}) async-start(f32[128,2,4]{2,1,0:T(2,128)} %bitcast.1), calls=%async_computation | async-start | bytes 262144 | tf_op jit(solution)/shard_map/all_to_all | solution.py:79
  13.7 2.1 %fusion = f32[4,256]{1,0:T(4,128)S(1)} fusion(bf16[4,256,1024]{2,1,0:T(8,128)(2,1)} %param.7), kind=kLoop, calls=%fused_computation.10 | loop fusion | flops 3144704 | bytes 2101248 | tf_op jit(solution)/shard_map/reduce_sum | solution.py:87
  15.8 3.5 %fusion.2.x_ref = bf16[4,256,1024]{2,1,0:T(8,128)(2,1)} fusion(bf16[4,256,1024]{2,1,0:T(8,128)(2,1)} %param.7, f32[1024]{0:T(1024)S(1)} %bitcast.93, f32[4,256]{1,0:T(4,128)S(1)} %add_rsqrt_fusion.3), kind=kLoop, calls=%fused_computation.12 | loop fusion | flops 4194304 | bytes 4202496 | tf_op jit(solution)/shard_map/convert_element_type | solution.py:88
  19.3 1.0 copy.66.m_ref
  20.3 10.5 %shard_map.73 = f32[128,8,256]{2,1,0:T(8,128)} custom-call(bf16[4,256,1024]{2,1,0:T(8,128)(2,1)} %fusion.2.x_ref, f32[4,256,1]{2,1,0:T(8,128)} %copy.66.m_ref, bf16[2,1024,3072]{2,1,0:T(8,128)(2,1)} %wv_ref.3, bf16[2,1024,3072]{2,1,0:T(8,128)(2,1)} %wv_ref.3), custom_call_target="tpu_custom_call" | custom-call | tf_op jit(solution)/shard_map/pallas_call | solution.py:52
  30.8 9.8 %all-to-all-start.1 = ((f32[128,8,256]{2,1,0:T(8,128)}), f32[128,8,256]{2,1,0:T(8,128)S(1)}, u32[]{:S(2)}, u32[]{:S(2)}) async-start(f32[128,8,256]{2,1,0:T(8,128)} %shard_map.73), calls=%async_computation.1 | async-start | bytes 2097152 | tf_op jit(solution)/shard_map/all_to_all | solution.py:90
  40.6 6.3 %fusion.10 = bf16[1024,1024]{1,0:T(8,128)(2,1)} fusion(bf16[1024,1024]{1,0:T(8,128)(2,1)S(1)} %bitcast.82, bf16[2,1024,3072]{2,1,0:T(8,128)(2,1)} %wv_ref.3), kind=kOutput, calls=%fused_computation.20 | convolution fusion | flops 2152726528 | bytes 6291456 | tf_op jit(solution)/shard_map/dot_general | solution.py:102
  47.0 4.0 %copy.68 = bf16[1024,1024]{0,1:T(8,128)(2,1)} copy(bf16[1024,1024]{1,0:T(8,128)(2,1)} %fusion.10) | data formatting | bytes 4194304 | tf_op jit(solution)/shard_map/convert_element_type | solution.py:105
  50.9 3.3 %reshape.166 = bf16[4,256,16,64]{1,0,3,2:T(4,128)(2,1)S(1)} reshape(bf16[1024,1024]{0,1:T(8,128)(2,1)} %copy.68) | data formatting | bytes 4194304 | tf_op jit(solution)/shard_map/reshape | solution.py:106
  54.8 2.2 %fusion.21 = (f32[64,64]{1,0:T(8,128)S(1)}, f32[64,64]{1,0:T(8,128)S(1)}) fusion(f32[64]{0:T(128)S(1)} %broadcast_in_dim.75, pred[64,64]{1,0:T(8,128)(4,1)S(1)} %get-tuple-element.28, pred[64,64]{1,0:T(8,128)(4,1)S(1)} %get-tuple-element.27, f32[64]{0:T(128)S(1)} %broadcast_in_dim.68), kind=kLoop, calls=%fused_computation.37 | loop fusion | flops 1302528 | bytes 41472 | tf_op jit(solution)/shard_map/reduce_prod | solution.py:99
  57.0 2.4 %all-to-all-done.1 = f32[128,8,256]{2,1,0:T(8,128)S(1)} async-done(((f32[128,8,256]{2,1,0:T(8,128)}), f32[128,8,256]{2,1,0:T(8,128)S(1)}, u32[]{:S(2)}, u32[]{:S(2)}) %all-to-all-start.1) | async-done | bytes 1048608 | tf_op jit(solution)/shard_map/all_to_all | solution.py:90
  60.1 0.9 broadcast_in_dim.74
  61.0 7.4 %all-to-all-start.2 = ((bf16[128,4,512]{2,1,0:T(4,128)(2,1)}), bf16[128,4,512]{2,1,0:T(4,128)(2,1)S(1)}, u32[]{:S(2)}, u32[]{:S(2)}) async-start(bf16[128,4,512]{2,1,0:T(4,128)(2,1)} %bitcast.10), calls=%async_computation.2 | async-start | bytes 1048576 | tf_op jit(solution)/shard_map/all_to_all | solution.py:113
  68.5 13.4 %all-to-all-done.2 = bf16[128,4,512]{2,1,0:T(4,128)(2,1)S(1)} async-done(((bf16[128,4,512]{2,1,0:T(4,128)(2,1)}), bf16[128,4,512]{2,1,0:T(4,128)(2,1)S(1)}, u32[]{:S(2)}, u32[]{:S(2)}) %all-to-all-start.2) | async-done | bytes 524320 | tf_op jit(solution)/shard_map/all_to_all | solution.py:113
  82.8 1.6 %reshape.168 = bf16[4,16,64,64]{3,2,1,0:T(8,128)(2,1)S(1)} reshape(bf16[4,128,512]{2,1,0:T(8,128)(2,1)} %copy.69) | data formatting | bytes 1048576 | tf_op jit(solution)/shard_map/reshape | solution.py:114
  86.0 1.0 copy-done.2
  87.0 1.2 copy-done.7
  88.2 2.7 %fusion.4 = (f32[4,256]{1,0:T(4,128)S(1)}, bf16[4,256,1024]{2,1,0:T(8,128)(2,1)S(1)}) fusion(bf16[4,256,1024]{1,2,0:T(8,128)(2,1)S(1)} %bitcast.84, bf16[2,1024,1024]{2,1,0:T(8,128)(2,1)S(1)} %copy-done.7, bf16[4,256,1024]{2,1,0:T(8,128)(2,1)S(1)} %copy-done.2), kind=kOutput, calls=%fused_computation.14 | convolution fusion | flops 2153774080 | bytes 8392704 | tf_op jit(solution)/shard_map/dot_general | solution.py:122
  91.0 1.3 copy-done.3
  92.3 1.9 %fusion.6.x_ref = bf16[4,256,1024]{2,1,0:T(8,128)(2,1)} fusion(bf16[4,256,1024]{2,1,0:T(8,128)(2,1)S(1)} %get-tuple-element.24, f32[1024]{0:T(1024)S(1)} %bitcast.92, f32[4,256]{1,0:T(4,128)S(1)} %add_rsqrt_fusion.2), kind=kLoop, calls=%fused_computation.16 | loop fusion | flops 4194304 | bytes 4202496 | tf_op jit(solution)/shard_map/convert_element_type | solution.py:88
  94.2 10.5 %shard_map.74 = f32[128,8,256]{2,1,0:T(8,128)} custom-call(bf16[4,256,1024]{2,1,0:T(8,128)(2,1)} %fusion.6.x_ref, f32[4,256,1]{2,1,0:T(8,128)} %copy.66.m_ref, bf16[2,1024,3072]{2,1,0:T(8,128)(2,1)} %wv_ref.3, bf16[2,1024,3072]{2,1,0:T(8,128)(2,1)} %wv_ref.3), custom_call_target="tpu_custom_call" | custom-call | tf_op jit(solution)/shard_map/pallas_call | solution.py:52
  104.7 4.5 %all-to-all-start.3 = ((f32[128,8,256]{2,1,0:T(8,128)}), f32[128,8,256]{2,1,0:T(8,128)S(1)}, u32[]{:S(2)}, u32[]{:S(2)}) async-start(f32[128,8,256]{2,1,0:T(8,128)} %shard_map.74), calls=%async_computation.3 | async-start | bytes 2097152 | tf_op jit(solution)/shard_map/all_to_all | solution.py:90
  109.2 6.4 %fusion.13 = bf16[1024,1024]{1,0:T(8,128)(2,1)} fusion(bf16[1024,1024]{1,0:T(8,128)(2,1)S(1)} %bitcast.83, bf16[2,1024,3072]{2,1,0:T(8,128)(2,1)} %wv_ref.3), kind=kOutput, calls=%fused_computation.23 | convolution fusion | flops 2152726528 | bytes 6291456 | tf_op jit(solution)/shard_map/dot_general | solution.py:102
  115.6 4.0 %copy.76 = bf16[1024,1024]{0,1:T(8,128)(2,1)} copy(bf16[1024,1024]{1,0:T(8,128)(2,1)} %fusion.13) | data formatting | bytes 4194304 | tf_op jit(solution)/shard_map/convert_element_type | solution.py:105
  119.5 3.3 %reshape.173 = bf16[4,256,16,64]{1,0,3,2:T(4,128)(2,1)S(1)} reshape(bf16[1024,1024]{0,1:T(8,128)(2,1)} %copy.76) | data formatting | bytes 4194304 | tf_op jit(solution)/shard_map/reshape | solution.py:106
  122.9 5.2 %all-to-all-done.3 = f32[128,8,256]{2,1,0:T(8,128)S(1)} async-done(((f32[128,8,256]{2,1,0:T(8,128)}), f32[128,8,256]{2,1,0:T(8,128)S(1)}, u32[]{:S(2)}, u32[]{:S(2)}) %all-to-all-start.3) | async-done | bytes 1048608 | tf_op jit(solution)/shard_map/all_to_all | solution.py:90
  129.6 5.0 %all-to-all-start.4 = ((bf16[128,4,512]{2,1,0:T(4,128)(2,1)}), bf16[128,4,512]{2,1,0:T(4,128)(2,1)S(1)}, u32[]{:S(2)}, u32[]{:S(2)}) async-start(bf16[128,4,512]{2,1,0:T(4,128)(2,1)} %bitcast.21), calls=%async_computation.4 | async-start | bytes 1048576 | tf_op jit(solution)/shard_map/all_to_all | solution.py:113
  134.7 13.6 %all-to-all-done.4 = bf16[128,4,512]{2,1,0:T(4,128)(2,1)S(1)} async-done(((bf16[128,4,512]{2,1,0:T(4,128)(2,1)}), bf16[128,4,512]{2,1,0:T(4,128)(2,1)S(1)}, u32[]{:S(2)}, u32[]{:S(2)}) %all-to-all-start.4) | async-done | bytes 524320 | tf_op jit(solution)/shard_map/all_to_all | solution.py:113
  149.2 1.6 %reshape.175 = bf16[4,16,64,64]{3,2,1,0:T(8,128)(2,1)S(1)} reshape(bf16[4,128,512]{2,1,0:T(8,128)(2,1)} %copy.77) | data formatting | bytes 1048576 | tf_op jit(solution)/shard_map/reshape | solution.py:114
  152.3 1.0 copy-done.4
  153.3 1.2 copy-done.8
  154.6 3.7 %fusion.7 = bf16[4,256,1024]{2,1,0:T(8,128)(2,1)} fusion(bf16[4,256,1024]{2,1,0:T(8,128)(2,1)S(1)} %copy-done.4, bf16[4,256,1024]{1,2,0:T(8,128)(2,1)S(1)} %bitcast.85, bf16[2,1024,1024]{2,1,0:T(8,128)(2,1)S(1)} %copy-done.8), kind=kOutput, calls=%fused_computation.17 | convolution fusion | flops 2150629376 | bytes 8388608 | tf_op jit(solution)/shard_map/dot_general | solution.py:122
  (52 shorter events, 9.8 us)
Async XLA Ops:
  0.0 19.3 %copy-start.6 = (s32[4,256]{1,0:T(4,128)S(1)}, s32[4,256]{1,0:T(4,128)}, u32[]{:S(2)}) copy-start(s32[4,256]{1,0:T(4,128)} %param.8) | copy-start | bytes 12292
  1.5 29.4 %all-to-all-start = ((f32[128,2,4]{2,1,0:T(2,128)}), f32[128,2,4]{2,1,0:T(2,128)S(1)}, u32[]{:S(2)}, u32[]{:S(2)}) async-start(f32[128,2,4]{2,1,0:T(2,128)} %bitcast.1), calls=%async_computation | async-start | bytes 262144 | tf_op jit(solution)/shard_map/all_to_all | solution.py:79
  20.3 20.3 %copy-start = (bf16[4,256,1024]{2,1,0:T(8,128)(2,1)S(1)}, bf16[4,256,1024]{2,1,0:T(8,128)(2,1)}, u32[]{:S(2)}) copy-start(bf16[4,256,1024]{2,1,0:T(8,128)(2,1)} %fusion.2.x_ref) | copy-start | bytes 6291460
  30.8 28.6 %all-to-all-start.1 = ((f32[128,8,256]{2,1,0:T(8,128)}), f32[128,8,256]{2,1,0:T(8,128)S(1)}, u32[]{:S(2)}, u32[]{:S(2)}) async-start(f32[128,8,256]{2,1,0:T(8,128)} %shard_map.73), calls=%async_computation.1 | async-start | bytes 2097152 | tf_op jit(solution)/shard_map/all_to_all | solution.py:90
  50.9 17.5 %copy-start.5 = (f32[2,1024]{1,0:T(2,128)S(1)}, f32[2,1024]{1,0:T(2,128)}, u32[]{:S(2)}) copy-start(f32[2,1024]{1,0:T(2,128)} %param.12) | copy-start | bytes 24580
  61.0 20.9 %all-to-all-start.2 = ((bf16[128,4,512]{2,1,0:T(4,128)(2,1)}), bf16[128,4,512]{2,1,0:T(4,128)(2,1)S(1)}, u32[]{:S(2)}, u32[]{:S(2)}) async-start(bf16[128,4,512]{2,1,0:T(4,128)(2,1)} %bitcast.10), calls=%async_computation.2 | async-start | bytes 1048576 | tf_op jit(solution)/shard_map/all_to_all | solution.py:113
  85.4 1.6 %copy-start.2 = (bf16[4,256,1024]{2,1,0:T(8,128)(2,1)S(1)}, bf16[4,256,1024]{2,1,0:T(8,128)(2,1)}, u32[]{:S(2)}) copy-start(bf16[4,256,1024]{2,1,0:T(8,128)(2,1)} %param.7) | copy-start | bytes 6291460
  85.4 2.8 %copy-start.7 = (bf16[2,1024,1024]{2,1,0:T(8,128)(2,1)S(1)}, bf16[2,1024,1024]{2,1,0:T(8,128)(2,1)}, u32[]{:S(2)}) copy-start(bf16[2,1024,1024]{2,1,0:T(8,128)(2,1)} %param.10) | copy-start | bytes 12582916
  90.9 1.3 copy-start.3
  94.2 15.1 %copy-start.1 = (bf16[4,256,1024]{2,1,0:T(8,128)(2,1)S(1)}, bf16[4,256,1024]{2,1,0:T(8,128)(2,1)}, u32[]{:S(2)}) copy-start(bf16[4,256,1024]{2,1,0:T(8,128)(2,1)} %fusion.6.x_ref) | copy-start | bytes 6291460
  104.7 23.4 %all-to-all-start.3 = ((f32[128,8,256]{2,1,0:T(8,128)}), f32[128,8,256]{2,1,0:T(8,128)S(1)}, u32[]{:S(2)}, u32[]{:S(2)}) async-start(f32[128,8,256]{2,1,0:T(8,128)} %shard_map.74), calls=%async_computation.3 | async-start | bytes 2097152 | tf_op jit(solution)/shard_map/all_to_all | solution.py:90
  129.6 18.7 %all-to-all-start.4 = ((bf16[128,4,512]{2,1,0:T(4,128)(2,1)}), bf16[128,4,512]{2,1,0:T(4,128)(2,1)S(1)}, u32[]{:S(2)}, u32[]{:S(2)}) async-start(bf16[128,4,512]{2,1,0:T(4,128)(2,1)} %bitcast.21), calls=%async_computation.4 | async-start | bytes 1048576 | tf_op jit(solution)/shard_map/all_to_all | solution.py:113
  151.7 1.6 %copy-start.4 = (bf16[4,256,1024]{2,1,0:T(8,128)(2,1)S(1)}, bf16[4,256,1024]{2,1,0:T(8,128)(2,1)}, u32[]{:S(2)}) copy-start(bf16[4,256,1024]{2,1,0:T(8,128)(2,1)} %copy-done.3) | copy-start | bytes 6291460
  151.7 2.8 %copy-start.8 = (bf16[2,1024,1024]{2,1,0:T(8,128)(2,1)S(1)}, bf16[2,1024,1024]{2,1,0:T(8,128)(2,1)}, u32[]{:S(2)}) copy-start(bf16[2,1024,1024]{2,1,0:T(8,128)(2,1)} %param.10) | copy-start | bytes 12582916

commit v2 on v1

--- a/solution.py
+++ b/solution.py
@@ -20,42 +20,47 @@
     rows = HEAD // per_head
     block = 4 * HEAD
 
+    step = 2
+
     def body(x_ref, m_ref, wk_ref, wv_ref, o_ref):
         t = pl.program_id(0)
-        x = x_ref[0]
+        x = x_ref[...].reshape(step * tokens, width)
         u = jnp.dot(x, wk_ref[0], preferred_element_type=jnp.float32)
-        key = jnp.where(u > 0, u + 1.0, jnp.exp(jnp.minimum(u, 0.0))) * m_ref[0]
+        key = jnp.where(u > 0, u + 1.0, jnp.exp(jnp.minimum(u, 0.0))) * m_ref[...].reshape(step * tokens, 1)
         key = key.astype(jnp.bfloat16)
         value = jnp.dot(x, wv_ref[0], preferred_element_type=jnp.float32).astype(jnp.bfloat16)
-        blocks = [
-            lax.dot_general(
-                key[:, b * block : (b + 1) * block],
-                value[:, b * block : (b + 1) * block],
-                (((0,), (0,)), ((), ())),
-                preferred_element_type=jnp.float32,
-            )
-            for b in range(width // block)
-        ]
-        for date in range(dates):
+        for sub in range(step):
+            rows_of = slice(sub * tokens, (sub + 1) * tokens)
+            blocks = [
+                lax.dot_general(
+                    key[rows_of, b * block : (b + 1) * block],
+                    value[rows_of, b * block : (b + 1) * block],
+                    (((0,), (0,)), ((), ())),
+                    preferred_element_type=jnp.float32,
+                )
+                for b in range(width // block)
+            ]
+            for first in range(0, dates, step):
 
-            @pl.when(t == date)
-            def _():
-                for b, kv in enumerate(blocks):
-                    for i in range(block // HEAD):
-                        h = b * (block // HEAD) + i
-                        for rb in range(per_head):
-                            o_ref[h * per_head + rb, :, date * HEAD : (date + 1) * HEAD] = kv[
-                                i * HEAD + rb * rows : i * HEAD + (rb + 1) * rows,
-                                i * HEAD : (i + 1) * HEAD,
-                            ]
+                @pl.when(t * step == first)
+                def _():
+                    date = first + sub
+                    for b, kv in enumerate(blocks):
+                        for i in range(block // HEAD):
+                            h = b * (block // HEAD) + i
+                            for rb in range(per_head):
+                                o_ref[h * per_head + rb, :, date * HEAD : (date + 1) * HEAD] = kv[
+                                    i * HEAD + rb * rows : i * HEAD + (rb + 1) * rows,
+                                    i * HEAD : (i + 1) * HEAD,
+                                ]
 
     return pl.pallas_call(
         body,
-        grid=(dates,),
+        grid=(dates // step,),
         out_shape=jax.ShapeDtypeStruct((n_dev, rows, dates * HEAD), jnp.float32),
         in_specs=[
-            pl.BlockSpec((1, tokens, width), lambda t: (t, 0, 0)),
-            pl.BlockSpec((1, tokens, 1), lambda t: (t, 0, 0)),
+            pl.BlockSpec((step, tokens, width), lambda t: (t, 0, 0)),
+            pl.BlockSpec((step, tokens, 1), lambda t: (t, 0, 0)),
             pl.BlockSpec((1, width, width), lambda t: (layer, 0, 1)),
             pl.BlockSpec((1, width, width), lambda t: (layer, 0, 2)),
         ],

time: 159 us -> 159 us (level)
  no operation moved by 1% of the time
where the time goes in v2:
time: 159 us; the launch traced here: 158 us
  starting transfers between devices  37.9 us (24%)
  waiting for transfers between devices  34.6 us (22%)
  local copies, waits for them, and re-layouts  31.8 us (20%)
  matrix products  21.4 us (13%)
  Pallas kernels  20.9 us (13%)
  other arithmetic  10.9 us (7%)
    all_to_all x2, waiting for transfers between devices, shards(): back = lax.all_to_all(outgoing, everyone, 0, 0, tiled=True)  27.1 us
    pallas_call x2, Pallas kernels, kv_chunks(): pl.pallas_call(body, grid=(dates // step,), out_shape=jax.ShapeDtypeStruc...  20.9 us
    all_to_all x2, starting transfers between devices, shards(): lax.all_to_all(kv_chunks(normalized_output, flag_f, qkv_weight, layer, n_...  14.3 us
    dot_general x2, matrix products, shards(): jnp.dot(flat, qkv_weight[layer, :, :width], preferred_element_type=jnp.fl...  12.7 us
    all_to_all x2, starting transfers between devices, shards(): back = lax.all_to_all(outgoing, everyone, 0, 0, tiled=True)  12.2 us
    all_to_all x1, starting transfers between devices, shards(): from_each = lax.all_to_all(to_each, everyone, 0, 0, tiled=True)  11.5 us
    convert_element_type x2, local copies, waits for them, and re-layouts, shards(): query = feature(proj_q).astype(jnp.bfloat16).reshape(dates_here, tokens_h...  7.9 us
    all_to_all x2, waiting for transfers between devices, shards(): lax.all_to_all(kv_chunks(normalized_output, flag_f, qkv_weight, layer, n_...  7.54 us
  transfers between devices with their start and end apart: 5, of which 4 were waited for; matrix products, arithmetic and copies ran while one was open for 24% of the time, Pallas kernels for 7%

profile of v2, /device:TPU:1, one launch (start us, length us, event | category | flops | bytes accessed | tf_op | source)
XLA Modules:
  0.0 157.9 jit_solution(6245844280158322116)
XLA Ops:
  1.5 11.5 %all-to-all-start = ((f32[128,2,4]{2,1,0:T(2,128)}), f32[128,2,4]{2,1,0:T(2,128)S(1)}, u32[]{:S(2)}, u32[]{:S(2)}) async-start(f32[128,2,4]{2,1,0:T(2,128)} %bitcast.1), calls=%async_computation | async-start | bytes 262144 | tf_op jit(solution)/shard_map/all_to_all | solution.py:84
  13.7 2.1 %fusion = f32[4,256]{1,0:T(4,128)S(1)} fusion(bf16[4,256,1024]{2,1,0:T(8,128)(2,1)} %param.7), kind=kLoop, calls=%fused_computation.10 | loop fusion | flops 3144704 | bytes 2101248 | tf_op jit(solution)/shard_map/reduce_sum | solution.py:92
  15.8 3.5 %fusion.2.x_ref = bf16[4,256,1024]{2,1,0:T(8,128)(2,1)} fusion(bf16[4,256,1024]{2,1,0:T(8,128)(2,1)} %param.7, f32[1024]{0:T(1024)S(1)} %bitcast.93, f32[4,256]{1,0:T(4,128)S(1)} %add_rsqrt_fusion.3), kind=kLoop, calls=%fused_computation.12 | loop fusion | flops 4194304 | bytes 4202496 | tf_op jit(solution)/shard_map/convert_element_type | solution.py:93
  19.3 1.0 copy.66.m_ref
  20.3 10.4 %shard_map.73 = f32[128,8,256]{2,1,0:T(8,128)} custom-call(bf16[4,256,1024]{2,1,0:T(8,128)(2,1)} %fusion.2.x_ref, f32[4,256,1]{2,1,0:T(8,128)} %copy.66.m_ref, bf16[2,1024,3072]{2,1,0:T(8,128)(2,1)} %wv_ref.3, bf16[2,1024,3072]{2,1,0:T(8,128)(2,1)} %wv_ref.3), custom_call_target="tpu_custom_call" | custom-call | tf_op jit(solution)/shard_map/pallas_call | solution.py:57
  30.7 9.8 %all-to-all-start.1 = ((f32[128,8,256]{2,1,0:T(8,128)}), f32[128,8,256]{2,1,0:T(8,128)S(1)}, u32[]{:S(2)}, u32[]{:S(2)}) async-start(f32[128,8,256]{2,1,0:T(8,128)} %shard_map.73), calls=%async_computation.1 | async-start | bytes 2097152 | tf_op jit(solution)/shard_map/all_to_all | solution.py:95
  40.5 6.3 %fusion.10 = bf16[1024,1024]{1,0:T(8,128)(2,1)} fusion(bf16[1024,1024]{1,0:T(8,128)(2,1)S(1)} %bitcast.82, bf16[2,1024,3072]{2,1,0:T(8,128)(2,1)} %wv_ref.3), kind=kOutput, calls=%fused_computation.20 | convolution fusion | flops 2152726528 | bytes 6291456 | tf_op jit(solution)/shard_map/dot_general | solution.py:107
  46.9 4.0 %copy.68 = bf16[1024,1024]{0,1:T(8,128)(2,1)} copy(bf16[1024,1024]{1,0:T(8,128)(2,1)} %fusion.10) | data formatting | bytes 4194304 | tf_op jit(solution)/shard_map/convert_element_type | solution.py:110
  50.8 3.3 %reshape.166 = bf16[4,256,16,64]{1,0,3,2:T(4,128)(2,1)S(1)} reshape(bf16[1024,1024]{0,1:T(8,128)(2,1)} %copy.68) | data formatting | bytes 4194304 | tf_op jit(solution)/shard_map/reshape | solution.py:111
  54.7 2.2 %fusion.21 = (f32[64,64]{1,0:T(8,128)S(1)}, f32[64,64]{1,0:T(8,128)S(1)}) fusion(f32[64]{0:T(128)S(1)} %broadcast_in_dim.75, pred[64,64]{1,0:T(8,128)(4,1)S(1)} %get-tuple-element.28, pred[64,64]{1,0:T(8,128)(4,1)S(1)} %get-tuple-element.27, f32[64]{0:T(128)S(1)} %broadcast_in_dim.68), kind=kLoop, calls=%fused_computation.37 | loop fusion | flops 1302528 | bytes 41472 | tf_op jit(solution)/shard_map/reduce_prod | solution.py:104
  56.9 2.4 %all-to-all-done.1 = f32[128,8,256]{2,1,0:T(8,128)S(1)} async-done(((f32[128,8,256]{2,1,0:T(8,128)}), f32[128,8,256]{2,1,0:T(8,128)S(1)}, u32[]{:S(2)}, u32[]{:S(2)}) %all-to-all-start.1) | async-done | bytes 1048608 | tf_op jit(solution)/shard_map/all_to_all | solution.py:95
  60.0 0.9 broadcast_in_dim.74
  60.9 7.4 %all-to-all-start.2 = ((bf16[128,4,512]{2,1,0:T(4,128)(2,1)}), bf16[128,4,512]{2,1,0:T(4,128)(2,1)S(1)}, u32[]{:S(2)}, u32[]{:S(2)}) async-start(bf16[128,4,512]{2,1,0:T(4,128)(2,1)} %bitcast.10), calls=%async_computation.2 | async-start | bytes 1048576 | tf_op jit(solution)/shard_map/all_to_all | solution.py:118
  68.4 13.4 %all-to-all-done.2 = bf16[128,4,512]{2,1,0:T(4,128)(2,1)S(1)} async-done(((bf16[128,4,512]{2,1,0:T(4,128)(2,1)}), bf16[128,4,512]{2,1,0:T(4,128)(2,1)S(1)}, u32[]{:S(2)}, u32[]{:S(2)}) %all-to-all-start.2) | async-done | bytes 524320 | tf_op jit(solution)/shard_map/all_to_all | solution.py:118
  82.7 1.6 %reshape.168 = bf16[4,16,64,64]{3,2,1,0:T(8,128)(2,1)S(1)} reshape(bf16[4,128,512]{2,1,0:T(8,128)(2,1)} %copy.69) | data formatting | bytes 1048576 | tf_op jit(solution)/shard_map/reshape | solution.py:119
  85.9 1.0 copy-done.2
  86.9 1.2 copy-done.7
  88.1 2.7 %fusion.4 = (f32[4,256]{1,0:T(4,128)S(1)}, bf16[4,256,1024]{2,1,0:T(8,128)(2,1)S(1)}) fusion(bf16[4,256,1024]{1,2,0:T(8,128)(2,1)S(1)} %bitcast.84, bf16[2,1024,1024]{2,1,0:T(8,128)(2,1)S(1)} %copy-done.7, bf16[4,256,1024]{2,1,0:T(8,128)(2,1)S(1)} %copy-done.2), kind=kOutput, calls=%fused_computation.14 | convolution fusion | flops 2153774080 | bytes 8392704 | tf_op jit(solution)/shard_map/dot_general | solution.py:127
  90.9 1.3 copy-done.3
  92.2 1.9 %fusion.6.x_ref = bf16[4,256,1024]{2,1,0:T(8,128)(2,1)} fusion(bf16[4,256,1024]{2,1,0:T(8,128)(2,1)S(1)} %get-tuple-element.24, f32[1024]{0:T(1024)S(1)} %bitcast.92, f32[4,256]{1,0:T(4,128)S(1)} %add_rsqrt_fusion.2), kind=kLoop, calls=%fused_computation.16 | loop fusion | flops 4194304 | bytes 4202496 | tf_op jit(solution)/shard_map/convert_element_type | solution.py:93
  94.1 10.4 %shard_map.74 = f32[128,8,256]{2,1,0:T(8,128)} custom-call(bf16[4,256,1024]{2,1,0:T(8,128)(2,1)} %fusion.6.x_ref, f32[4,256,1]{2,1,0:T(8,128)} %copy.66.m_ref, bf16[2,1024,3072]{2,1,0:T(8,128)(2,1)} %wv_ref.3, bf16[2,1024,3072]{2,1,0:T(8,128)(2,1)} %wv_ref.3), custom_call_target="tpu_custom_call" | custom-call | tf_op jit(solution)/shard_map/pallas_call | solution.py:57
  104.5 4.5 %all-to-all-start.3 = ((f32[128,8,256]{2,1,0:T(8,128)}), f32[128,8,256]{2,1,0:T(8,128)S(1)}, u32[]{:S(2)}, u32[]{:S(2)}) async-start(f32[128,8,256]{2,1,0:T(8,128)} %shard_map.74), calls=%async_computation.3 | async-start | bytes 2097152 | tf_op jit(solution)/shard_map/all_to_all | solution.py:95
  109.0 6.4 %fusion.13 = bf16[1024,1024]{1,0:T(8,128)(2,1)} fusion(bf16[1024,1024]{1,0:T(8,128)(2,1)S(1)} %bitcast.83, bf16[2,1024,3072]{2,1,0:T(8,128)(2,1)} %wv_ref.3), kind=kOutput, calls=%fused_computation.23 | convolution fusion | flops 2152726528 | bytes 6291456 | tf_op jit(solution)/shard_map/dot_general | solution.py:107
  115.4 4.0 %copy.76 = bf16[1024,1024]{0,1:T(8,128)(2,1)} copy(bf16[1024,1024]{1,0:T(8,128)(2,1)} %fusion.13) | data formatting | bytes 4194304 | tf_op jit(solution)/shard_map/convert_element_type | solution.py:110
  119.3 3.3 %reshape.173 = bf16[4,256,16,64]{1,0,3,2:T(4,128)(2,1)S(1)} reshape(bf16[1024,1024]{0,1:T(8,128)(2,1)} %copy.76) | data formatting | bytes 4194304 | tf_op jit(solution)/shard_map/reshape | solution.py:111
  122.7 5.1 %all-to-all-done.3 = f32[128,8,256]{2,1,0:T(8,128)S(1)} async-done(((f32[128,8,256]{2,1,0:T(8,128)}), f32[128,8,256]{2,1,0:T(8,128)S(1)}, u32[]{:S(2)}, u32[]{:S(2)}) %all-to-all-start.3) | async-done | bytes 1048608 | tf_op jit(solution)/shard_map/all_to_all | solution.py:95
  129.4 4.8 %all-to-all-start.4 = ((bf16[128,4,512]{2,1,0:T(4,128)(2,1)}), bf16[128,4,512]{2,1,0:T(4,128)(2,1)S(1)}, u32[]{:S(2)}, u32[]{:S(2)}) async-start(bf16[128,4,512]{2,1,0:T(4,128)(2,1)} %bitcast.21), calls=%async_computation.4 | async-start | bytes 1048576 | tf_op jit(solution)/shard_map/all_to_all | solution.py:118
  134.3 13.6 %all-to-all-done.4 = bf16[128,4,512]{2,1,0:T(4,128)(2,1)S(1)} async-done(((bf16[128,4,512]{2,1,0:T(4,128)(2,1)}), bf16[128,4,512]{2,1,0:T(4,128)(2,1)S(1)}, u32[]{:S(2)}, u32[]{:S(2)}) %all-to-all-start.4) | async-done | bytes 524320 | tf_op jit(solution)/shard_map/all_to_all | solution.py:118
  148.8 1.6 %reshape.175 = bf16[4,16,64,64]{3,2,1,0:T(8,128)(2,1)S(1)} reshape(bf16[4,128,512]{2,1,0:T(8,128)(2,1)} %copy.77) | data formatting | bytes 1048576 | tf_op jit(solution)/shard_map/reshape | solution.py:119
  151.9 1.0 copy-done.4
  152.9 1.2 copy-done.8
  154.2 3.7 %fusion.7 = bf16[4,256,1024]{2,1,0:T(8,128)(2,1)} fusion(bf16[4,256,1024]{2,1,0:T(8,128)(2,1)S(1)} %copy-done.4, bf16[4,256,1024]{1,2,0:T(8,128)(2,1)S(1)} %bitcast.85, bf16[2,1024,1024]{2,1,0:T(8,128)(2,1)S(1)} %copy-done.8), kind=kOutput, calls=%fused_computation.17 | convolution fusion | flops 2150629376 | bytes 8388608 | tf_op jit(solution)/shard_map/dot_general | solution.py:127
  (52 shorter events, 9.8 us)
Async XLA Ops:
  0.0 19.3 %copy-start.6 = (s32[4,256]{1,0:T(4,128)S(1)}, s32[4,256]{1,0:T(4,128)}, u32[]{:S(2)}) copy-start(s32[4,256]{1,0:T(4,128)} %param.8) | copy-start | bytes 12292
  1.5 29.3 %all-to-all-start = ((f32[128,2,4]{2,1,0:T(2,128)}), f32[128,2,4]{2,1,0:T(2,128)S(1)}, u32[]{:S(2)}, u32[]{:S(2)}) async-start(f32[128,2,4]{2,1,0:T(2,128)} %bitcast.1), calls=%async_computation | async-start | bytes 262144 | tf_op jit(solution)/shard_map/all_to_all | solution.py:84
  20.3 20.2 %copy-start = (bf16[4,256,1024]{2,1,0:T(8,128)(2,1)S(1)}, bf16[4,256,1024]{2,1,0:T(8,128)(2,1)}, u32[]{:S(2)}) copy-start(bf16[4,256,1024]{2,1,0:T(8,128)(2,1)} %fusion.2.x_ref) | copy-start | bytes 6291460
  30.7 28.6 %all-to-all-start.1 = ((f32[128,8,256]{2,1,0:T(8,128)}), f32[128,8,256]{2,1,0:T(8,128)S(1)}, u32[]{:S(2)}, u32[]{:S(2)}) async-start(f32[128,8,256]{2,1,0:T(8,128)} %shard_map.73), calls=%async_computation.1 | async-start | bytes 2097152 | tf_op jit(solution)/shard_map/all_to_all | solution.py:95
  50.8 17.5 %copy-start.5 = (f32[2,1024]{1,0:T(2,128)S(1)}, f32[2,1024]{1,0:T(2,128)}, u32[]{:S(2)}) copy-start(f32[2,1024]{1,0:T(2,128)} %param.12) | copy-start | bytes 24580
  60.9 21.0 %all-to-all-start.2 = ((bf16[128,4,512]{2,1,0:T(4,128)(2,1)}), bf16[128,4,512]{2,1,0:T(4,128)(2,1)S(1)}, u32[]{:S(2)}, u32[]{:S(2)}) async-start(bf16[128,4,512]{2,1,0:T(4,128)(2,1)} %bitcast.10), calls=%async_computation.2 | async-start | bytes 1048576 | tf_op jit(solution)/shard_map/all_to_all | solution.py:118
  85.3 1.6 %copy-start.2 = (bf16[4,256,1024]{2,1,0:T(8,128)(2,1)S(1)}, bf16[4,256,1024]{2,1,0:T(8,128)(2,1)}, u32[]{:S(2)}) copy-start(bf16[4,256,1024]{2,1,0:T(8,128)(2,1)} %param.7) | copy-start | bytes 6291460
  85.3 2.8 %copy-start.7 = (bf16[2,1024,1024]{2,1,0:T(8,128)(2,1)S(1)}, bf16[2,1024,1024]{2,1,0:T(8,128)(2,1)}, u32[]{:S(2)}) copy-start(bf16[2,1024,1024]{2,1,0:T(8,128)(2,1)} %param.10) | copy-start | bytes 12582916
  90.8 1.3 copy-start.3
  94.1 15.0 %copy-start.1 = (bf16[4,256,1024]{2,1,0:T(8,128)(2,1)S(1)}, bf16[4,256,1024]{2,1,0:T(8,128)(2,1)}, u32[]{:S(2)}) copy-start(bf16[4,256,1024]{2,1,0:T(8,128)(2,1)} %fusion.6.x_ref) | copy-start | bytes 6291460
  104.5 23.4 %all-to-all-start.3 = ((f32[128,8,256]{2,1,0:T(8,128)}), f32[128,8,256]{2,1,0:T(8,128)S(1)}, u32[]{:S(2)}, u32[]{:S(2)}) async-start(f32[128,8,256]{2,1,0:T(8,128)} %shard_map.74), calls=%async_computation.3 | async-start | bytes 2097152 | tf_op jit(solution)/shard_map/all_to_all | solution.py:95
  129.4 18.5 %all-to-all-start.4 = ((bf16[128,4,512]{2,1,0:T(4,128)(2,1)}), bf16[128,4,512]{2,1,0:T(4,128)(2,1)S(1)}, u32[]{:S(2)}, u32[]{:S(2)}) async-start(bf16[128,4,512]{2,1,0:T(4,128)(2,1)} %bitcast.21), calls=%async_computation.4 | async-start | bytes 1048576 | tf_op jit(solution)/shard_map/all_to_all | solution.py:118
  151.3 1.6 %copy-start.4 = (bf16[4,256,1024]{2,1,0:T(8,128)(2,1)S(1)}, bf16[4,256,1024]{2,1,0:T(8,128)(2,1)}, u32[]{:S(2)}) copy-start(bf16[4,256,1024]{2,1,0:T(8,128)(2,1)} %copy-done.3) | copy-start | bytes 6291460
  151.3 2.8 %copy-start.8 = (bf16[2,1024,1024]{2,1,0:T(8,128)(2,1)S(1)}, bf16[2,1024,1024]{2,1,0:T(8,128)(2,1)}, u32[]{:S(2)}) copy-start(bf16[2,1024,1024]{2,1,0:T(8,128)(2,1)} %param.10) | copy-start | bytes 12582916

commit v3 on v1

--- a/solution.py
+++ b/solution.py
@@ -14,15 +14,17 @@
     return jax.nn.elu(u) + 1.0
 
 
-def kv_chunks(normed, flags, weights, layer, n_dev):
-    dates, tokens, width = normed.shape
+def kv_chunks(tokens_in, gain, flags, weights, layer, n_dev):
+    dates, tokens, width = tokens_in.shape
     per_head = n_dev // HEADS
     rows = HEAD // per_head
     block = 4 * HEAD
 
-    def body(x_ref, m_ref, wk_ref, wv_ref, o_ref):
+    def body(x_ref, g_ref, m_ref, wk_ref, wv_ref, o_ref):
         t = pl.program_id(0)
-        x = x_ref[0]
+        xf = x_ref[0].astype(jnp.float32)
+        in_msq = jnp.mean(xf * xf, -1, keepdims=True) + 1e-05
+        x = (xf * lax.rsqrt(in_msq) * g_ref[...]).astype(jnp.bfloat16)
         u = jnp.dot(x, wk_ref[0], preferred_element_type=jnp.float32)
         key = jnp.where(u > 0, u + 1.0, jnp.exp(jnp.minimum(u, 0.0))) * m_ref[0]
         key = key.astype(jnp.bfloat16)
@@ -55,13 +57,14 @@
         out_shape=jax.ShapeDtypeStruct((n_dev, rows, dates * HEAD), jnp.float32),
         in_specs=[
             pl.BlockSpec((1, tokens, width), lambda t: (t, 0, 0)),
+            pl.BlockSpec((1, width), lambda t: (0, 0)),
             pl.BlockSpec((1, tokens, 1), lambda t: (t, 0, 0)),
             pl.BlockSpec((1, width, width), lambda t: (layer, 0, 1)),
             pl.BlockSpec((1, width, width), lambda t: (layer, 0, 2)),
         ],
         out_specs=pl.BlockSpec((n_dev, rows, dates * HEAD), lambda t: (0, 0, 0)),
         compiler_params=pltpu.CompilerParams(dimension_semantics=("arbitrary",)),
-    )(normed, flags, weights, weights)
+    )(tokens_in, gain, flags, weights, weights)
 
 
 def shards(frames, cloud_mask, qkv_weight, out_weight, norm_gain, head_norm_scale, decay):
@@ -88,7 +91,7 @@
         normalized_output = (xf * lax.rsqrt(in_msq) * norm_gain[layer]).astype(jnp.bfloat16)
         flat = normalized_output.reshape(-1, width)
         pieces = lax.all_to_all(
-            kv_chunks(normalized_output, flag_f, qkv_weight, layer, n_dev), everyone, 0, 0, tiled=True
+            kv_chunks(current, norm_gain[layer][None, :], flag_f, qkv_weight, layer, n_dev), everyone, 0, 0, tiled=True
         )
         rows = pieces.shape[1]
         kv = pieces.reshape(n_date, n_space, rows, dates_here * HEAD).sum(1)

time: 159 us -> 157 us (0.987)
  other arithmetic: 10.9 us -> 8.21 us
  waiting for transfers between devices: 34.6 us -> 36.7 us
  local copies, waits for them, and re-layouts: 31.8 us -> 29.8 us
    convert_element_type x2, other arithmetic: 5.35 us -> 2.67 us  [shards(): (xf * lax.rsqrt(in_msq) * norm_gain[layer]).astype(jnp.bfloat16)]
    all_to_all x2, waiting for transfers between devices: 7.56 us -> 9.68 us  [shards(): lax.all_to_all(kv_chunks(current, norm_gain[layer][None, :], flag_f, qkv_...]
  transfers between devices with their start and end apart: 5 -> 5, of which waited for: 4 -> 4; matrix products, arithmetic and copies ran while one was open for 24% -> 22% of each run, Pallas kernels for 7% -> 7%
where the time goes in v3:
time: 157 us; the launch traced here: 156 us
  starting transfers between devices  37.9 us (24%)
  waiting for transfers between devices  36.7 us (23%)
  local copies, waits for them, and re-layouts  29.8 us (19%)
  Pallas kernels  21.9 us (14%)
  matrix products  21.4 us (14%)
  other arithmetic  8.21 us (5%)
    all_to_all x2, waiting for transfers between devices, shards(): back = lax.all_to_all(outgoing, everyone, 0, 0, tiled=True)  27.1 us
    pallas_call x2, Pallas kernels, kv_chunks(): pl.pallas_call(body, grid=(dates,), out_shape=jax.ShapeDtypeStruct((n_dev...  21.9 us
    all_to_all x2, starting transfers between devices, shards(): lax.all_to_all(kv_chunks(current, norm_gain[layer][None, :], flag_f, qkv_...  14.3 us
    all_to_all x2, starting transfers between devices, shards(): back = lax.all_to_all(outgoing, everyone, 0, 0, tiled=True)  12.1 us
    all_to_all x1, starting transfers between devices, shards(): from_each = lax.all_to_all(to_each, everyone, 0, 0, tiled=True)  11.5 us
    dot_general x2, matrix products, shards(): jnp.dot(flat, qkv_weight[layer, :, :width], preferred_element_type=jnp.fl...  11.4 us
    all_to_all x2, waiting for transfers between devices, shards(): lax.all_to_all(kv_chunks(current, norm_gain[layer][None, :], flag_f, qkv_...  9.68 us
    dot_general x2, matrix products, shards(): jnp.dot(mixed.reshape(-1, width), out_weight[layer], preferred_element_ty...  7.64 us
  transfers between devices with their start and end apart: 5, of which 4 were waited for; matrix products, arithmetic and copies ran while one was open for 22% of the time, Pallas kernels for 7%

profile of v3, /device:TPU:1, one launch (start us, length us, event | category | flops | bytes accessed | tf_op | source)
XLA Modules:
  0.0 156.1 jit_solution(3919027641043999381)
XLA Ops:
  1.5 11.5 %all-to-all-start = ((f32[128,2,4]{2,1,0:T(2,128)}), f32[128,2,4]{2,1,0:T(2,128)S(1)}, u32[]{:S(2)}, u32[]{:S(2)}) async-start(f32[128,2,4]{2,1,0:T(2,128)} %bitcast.1), calls=%async_computation | async-start | bytes 262144 | tf_op jit(solution)/shard_map/all_to_all | solution.py:82
  13.0 1.4 fusion.54
  14.3 2.1 %fusion = f32[4,256]{1,0:T(4,128)S(1)} fusion(bf16[4,256,1024]{2,1,0:T(8,128)(2,1)} %x_ref.1), kind=kLoop, calls=%fused_computation.10 | loop fusion | flops 3144704 | bytes 2101248 | tf_op jit(solution)/shard_map/reduce_sum | solution.py:90
  16.4 2.1 %fusion.2 = bf16[4,256,1024]{2,1,0:T(8,128)(2,1)S(1)} fusion(bf16[4,256,1024]{2,1,0:T(8,128)(2,1)} %x_ref.1, f32[1024]{0:T(1024)S(1)} %bitcast.92, f32[4,256]{1,0:T(4,128)S(1)} %add_rsqrt_fusion.3), kind=kLoop, calls=%fused_computation.12 | loop fusion | flops 4194304 | bytes 4202496 | tf_op jit(solution)/shard_map/convert_element_type | solution.py:91
  18.6 1.0 copy.66.m_ref
  19.6 10.9 %shard_map.73 = f32[128,8,256]{2,1,0:T(8,128)} custom-call(bf16[4,256,1024]{2,1,0:T(8,128)(2,1)} %x_ref.1, f32[1,1024]{1,0:T(1,128)} %copy-done.4, f32[4,256,1]{2,1,0:T(8,128)} %copy.66.m_ref, bf16[2,1024,3072]{2,1,0:T(8,128)(2,1)} %wv_ref.3, bf16[2,1024,3072]{2,1,0:T(8,128)(2,1)} %wv_ref.3), custom_call_target="tpu_custom_call" | custom-call | tf_op jit(solution)/shard_map/pallas_call | solution.py:54
  30.5 9.7 %all-to-all-start.1 = ((f32[128,8,256]{2,1,0:T(8,128)}), f32[128,8,256]{2,1,0:T(8,128)S(1)}, u32[]{:S(2)}, u32[]{:S(2)}) async-start(f32[128,8,256]{2,1,0:T(8,128)} %shard_map.73), calls=%async_computation.1 | async-start | bytes 2097152 | tf_op jit(solution)/shard_map/all_to_all | solution.py:93
  40.2 6.3 %fusion.10 = bf16[1024,1024]{1,0:T(8,128)(2,1)} fusion(bf16[1024,1024]{1,0:T(8,128)(2,1)S(1)} %bitcast.82, bf16[2,1024,3072]{2,1,0:T(8,128)(2,1)} %wv_ref.3), kind=kOutput, calls=%fused_computation.20 | convolution fusion | flops 2152726528 | bytes 6291456 | tf_op jit(solution)/shard_map/dot_general | solution.py:105
  46.6 4.0 %copy.68 = bf16[1024,1024]{0,1:T(8,128)(2,1)} copy(bf16[1024,1024]{1,0:T(8,128)(2,1)} %fusion.10) | data formatting | bytes 4194304 | tf_op jit(solution)/shard_map/convert_element_type | solution.py:108
  50.5 3.3 %reshape.166 = bf16[4,256,16,64]{1,0,3,2:T(4,128)(2,1)S(1)} reshape(bf16[1024,1024]{0,1:T(8,128)(2,1)} %copy.68) | data formatting | bytes 4194304 | tf_op jit(solution)/shard_map/reshape | solution.py:109
  54.4 2.2 %fusion.21 = (f32[64,64]{1,0:T(8,128)S(1)}, f32[64,64]{1,0:T(8,128)S(1)}) fusion(f32[64]{0:T(128)S(1)} %broadcast_in_dim.75, pred[64,64]{1,0:T(8,128)(4,1)S(1)} %get-tuple-element.28, pred[64,64]{1,0:T(8,128)(4,1)S(1)} %get-tuple-element.27, f32[64]{0:T(128)S(1)} %broadcast_in_dim.68), kind=kLoop, calls=%fused_computation.37 | loop fusion | flops 1302528 | bytes 41472 | tf_op jit(solution)/shard_map/reduce_prod | solution.py:102
  56.6 2.4 %all-to-all-done.1 = f32[128,8,256]{2,1,0:T(8,128)S(1)} async-done(((f32[128,8,256]{2,1,0:T(8,128)}), f32[128,8,256]{2,1,0:T(8,128)S(1)}, u32[]{:S(2)}, u32[]{:S(2)}) %all-to-all-start.1) | async-done | bytes 1048608 | tf_op jit(solution)/shard_map/all_to_all | solution.py:93
  59.7 0.9 broadcast_in_dim.74
  60.6 7.4 %all-to-all-start.2 = ((bf16[128,4,512]{2,1,0:T(4,128)(2,1)}), bf16[128,4,512]{2,1,0:T(4,128)(2,1)S(1)}, u32[]{:S(2)}, u32[]{:S(2)}) async-start(bf16[128,4,512]{2,1,0:T(4,128)(2,1)} %bitcast.10), calls=%async_computation.2 | async-start | bytes 1048576 | tf_op jit(solution)/shard_map/all_to_all | solution.py:116
  68.1 13.4 %all-to-all-done.2 = bf16[128,4,512]{2,1,0:T(4,128)(2,1)S(1)} async-done(((bf16[128,4,512]{2,1,0:T(4,128)(2,1)}), bf16[128,4,512]{2,1,0:T(4,128)(2,1)S(1)}, u32[]{:S(2)}, u32[]{:S(2)}) %all-to-all-start.2) | async-done | bytes 524320 | tf_op jit(solution)/shard_map/all_to_all | solution.py:116
  82.4 1.6 %reshape.168 = bf16[4,16,64,64]{3,2,1,0:T(8,128)(2,1)S(1)} reshape(bf16[4,128,512]{2,1,0:T(8,128)(2,1)} %copy.69) | data formatting | bytes 1048576 | tf_op jit(solution)/shard_map/reshape | solution.py:117
  85.6 1.0 copy-done
  86.6 1.2 copy-done.7
  87.8 3.9 %fusion.4 = (f32[4,256]{1,0:T(4,128)S(1)}, bf16[4,256,1024]{2,1,0:T(8,128)(2,1)}) fusion(bf16[4,256,1024]{1,2,0:T(8,128)(2,1)S(1)} %bitcast.83, bf16[2,1024,1024]{2,1,0:T(8,128)(2,1)S(1)} %copy-done.7, bf16[4,256,1024]{2,1,0:T(8,128)(2,1)S(1)} %copy-done), kind=kOutput, calls=%fused_computation.14 | convolution fusion | flops 2153774080 | bytes 8392704 | tf_op jit(solution)/shard_map/dot_general | solution.py:125
  91.8 11.0 %shard_map.74 = f32[128,8,256]{2,1,0:T(8,128)} custom-call(bf16[4,256,1024]{2,1,0:T(8,128)(2,1)} %get-tuple-element.24.x_ref, f32[1,1024]{1,0:T(1,128)} %get-tuple-element.17.g_ref, f32[4,256,1]{2,1,0:T(8,128)} %copy.66.m_ref, bf16[2,1024,3072]{2,1,0:T(8,128)(2,1)} %wv_ref.3, bf16[2,1024,3072]{2,1,0:T(8,128)(2,1)} %wv_ref.3), custom_call_target="tpu_custom_call" | custom-call | tf_op jit(solution)/shard_map/pallas_call | solution.py:54
  102.8 4.5 %all-to-all-start.3 = ((f32[128,8,256]{2,1,0:T(8,128)}), f32[128,8,256]{2,1,0:T(8,128)S(1)}, u32[]{:S(2)}, u32[]{:S(2)}) async-start(f32[128,8,256]{2,1,0:T(8,128)} %shard_map.74), calls=%async_computation.3 | async-start | bytes 2097152 | tf_op jit(solution)/shard_map/all_to_all | solution.py:93
  107.9 5.0 %fusion.13 = bf16[1024,1024]{1,0:T(8,128)(2,1)S(1)} fusion(bf16[1024,1024]{1,0:T(8,128)(2,1)S(1)} %bitcast.85, bf16[2,1024,3072]{2,1,0:T(8,128)(2,1)} %wv_ref.3), kind=kOutput, calls=%fused_computation.23 | convolution fusion | flops 2152726528 | bytes 6291456 | tf_op jit(solution)/shard_map/dot_general | solution.py:105
  112.9 2.6 %copy.76 = bf16[1024,1024]{0,1:T(8,128)(2,1)} copy(bf16[1024,1024]{1,0:T(8,128)(2,1)S(1)} %fusion.13) | data formatting | bytes 4194304 | tf_op jit(solution)/shard_map/convert_element_type | solution.py:108
  115.5 3.3 %reshape.173 = bf16[4,256,16,64]{1,0,3,2:T(4,128)(2,1)S(1)} reshape(bf16[1024,1024]{0,1:T(8,128)(2,1)} %copy.76) | data formatting | bytes 4194304 | tf_op jit(solution)/shard_map/reshape | solution.py:109
  118.8 7.3 %all-to-all-done.3 = f32[128,8,256]{2,1,0:T(8,128)S(1)} async-done(((f32[128,8,256]{2,1,0:T(8,128)}), f32[128,8,256]{2,1,0:T(8,128)S(1)}, u32[]{:S(2)}, u32[]{:S(2)}) %all-to-all-start.3) | async-done | bytes 1048608 | tf_op jit(solution)/shard_map/all_to_all | solution.py:93
  126.8 0.9 broadcast_in_dim.78
  127.7 4.7 %all-to-all-start.4 = ((bf16[128,4,512]{2,1,0:T(4,128)(2,1)}), bf16[128,4,512]{2,1,0:T(4,128)(2,1)S(1)}, u32[]{:S(2)}, u32[]{:S(2)}) async-start(bf16[128,4,512]{2,1,0:T(4,128)(2,1)} %bitcast.21), calls=%async_computation.4 | async-start | bytes 1048576 | tf_op jit(solution)/shard_map/all_to_all | solution.py:116
  132.5 13.6 %all-to-all-done.4 = bf16[128,4,512]{2,1,0:T(4,128)(2,1)S(1)} async-done(((bf16[128,4,512]{2,1,0:T(4,128)(2,1)}), bf16[128,4,512]{2,1,0:T(4,128)(2,1)S(1)}, u32[]{:S(2)}, u32[]{:S(2)}) %all-to-all-start.4) | async-done | bytes 524320 | tf_op jit(solution)/shard_map/all_to_all | solution.py:116
  147.0 1.6 %reshape.175 = bf16[4,16,64,64]{3,2,1,0:T(8,128)(2,1)S(1)} reshape(bf16[4,128,512]{2,1,0:T(8,128)(2,1)} %copy.77) | data formatting | bytes 1048576 | tf_op jit(solution)/shard_map/reshape | solution.py:117
  150.2 1.0 copy-done.2
  151.2 1.2 copy-done.8
  152.4 3.7 %fusion.7 = bf16[4,256,1024]{2,1,0:T(8,128)(2,1)} fusion(bf16[4,256,1024]{2,1,0:T(8,128)(2,1)S(1)} %copy-done.2, bf16[4,256,1024]{1,2,0:T(8,128)(2,1)S(1)} %bitcast.84, bf16[2,1024,1024]{2,1,0:T(8,128)(2,1)S(1)} %copy-done.8), kind=kOutput, calls=%fused_computation.17 | convolution fusion | flops 2150629376 | bytes 8388608 | tf_op jit(solution)/shard_map/dot_general | solution.py:125
  (52 shorter events, 8.6 us)
Async XLA Ops:
  0.0 18.6 %copy-start.6 = (s32[4,256]{1,0:T(4,128)S(1)}, s32[4,256]{1,0:T(4,128)}, u32[]{:S(2)}) copy-start(s32[4,256]{1,0:T(4,128)} %param.8) | copy-start | bytes 12292
  1.5 29.0 %all-to-all-start = ((f32[128,2,4]{2,1,0:T(2,128)}), f32[128,2,4]{2,1,0:T(2,128)S(1)}, u32[]{:S(2)}, u32[]{:S(2)}) async-start(f32[128,2,4]{2,1,0:T(2,128)} %bitcast.1), calls=%async_computation | async-start | bytes 262144 | tf_op jit(solution)/shard_map/all_to_all | solution.py:82
  14.3 5.3 %copy-start.4 = (f32[1,1024]{1,0:T(1,128)}, f32[1,1024]{1,0:T(1,128)S(1)}, u32[]{:S(2)}) copy-start(f32[1,1024]{1,0:T(1,128)S(1)} %get-tuple-element.18.g_ref) | copy-start | bytes 12292
  30.5 28.5 %all-to-all-start.1 = ((f32[128,8,256]{2,1,0:T(8,128)}), f32[128,8,256]{2,1,0:T(8,128)S(1)}, u32[]{:S(2)}, u32[]{:S(2)}) async-start(f32[128,8,256]{2,1,0:T(8,128)} %shard_map.73), calls=%async_computation.1 | async-start | bytes 2097152 | tf_op jit(solution)/shard_map/all_to_all | solution.py:93
  50.5 17.5 %copy-start.5 = (f32[2,1024]{1,0:T(2,128)S(1)}, f32[2,1024]{1,0:T(2,128)}, u32[]{:S(2)}) copy-start(f32[2,1024]{1,0:T(2,128)} %param.12) | copy-start | bytes 24580
  60.6 20.9 %all-to-all-start.2 = ((bf16[128,4,512]{2,1,0:T(4,128)(2,1)}), bf16[128,4,512]{2,1,0:T(4,128)(2,1)S(1)}, u32[]{:S(2)}, u32[]{:S(2)}) async-start(bf16[128,4,512]{2,1,0:T(4,128)(2,1)} %bitcast.10), calls=%async_computation.2 | async-start | bytes 1048576 | tf_op jit(solution)/shard_map/all_to_all | solution.py:116
  85.0 1.6 %copy-start = (bf16[4,256,1024]{2,1,0:T(8,128)(2,1)S(1)}, bf16[4,256,1024]{2,1,0:T(8,128)(2,1)}, u32[]{:S(2)}) copy-start(bf16[4,256,1024]{2,1,0:T(8,128)(2,1)} %x_ref.1) | copy-start | bytes 6291460
  85.0 2.8 %copy-start.7 = (bf16[2,1024,1024]{2,1,0:T(8,128)(2,1)S(1)}, bf16[2,1024,1024]{2,1,0:T(8,128)(2,1)}, u32[]{:S(2)}) copy-start(bf16[2,1024,1024]{2,1,0:T(8,128)(2,1)} %param.10) | copy-start | bytes 12582916
  91.8 15.5 %copy-start.1 = (bf16[4,256,1024]{2,1,0:T(8,128)(2,1)S(1)}, bf16[4,256,1024]{2,1,0:T(8,128)(2,1)}, u32[]{:S(2)}) copy-start(bf16[4,256,1024]{2,1,0:T(8,128)(2,1)} %get-tuple-element.24.x_ref) | copy-start | bytes 6291460
  91.8 15.6 %copy-start.3 = (f32[1,1024]{1,0:T(1,128)S(1)}, f32[1,1024]{1,0:T(1,128)}, u32[]{:S(2)}) copy-start(f32[1,1024]{1,0:T(1,128)} %get-tuple-element.17.g_ref) | copy-start | bytes 12292
  102.8 23.4 %all-to-all-start.3 = ((f32[128,8,256]{2,1,0:T(8,128)}), f32[128,8,256]{2,1,0:T(8,128)S(1)}, u32[]{:S(2)}, u32[]{:S(2)}) async-start(f32[128,8,256]{2,1,0:T(8,128)} %shard_map.74), calls=%async_computation.3 | async-start | bytes 2097152 | tf_op jit(solution)/shard_map/all_to_all | solution.py:93
  127.7 18.4 %all-to-all-start.4 = ((bf16[128,4,512]{2,1,0:T(4,128)(2,1)}), bf16[128,4,512]{2,1,0:T(4,128)(2,1)S(1)}, u32[]{:S(2)}, u32[]{:S(2)}) async-start(bf16[128,4,512]{2,1,0:T(4,128)(2,1)} %bitcast.21), calls=%async_computation.4 | async-start | bytes 1048576 | tf_op jit(solution)/shard_map/all_to_all | solution.py:116
  149.6 1.6 %copy-start.2 = (bf16[4,256,1024]{2,1,0:T(8,128)(2,1)S(1)}, bf16[4,256,1024]{2,1,0:T(8,128)(2,1)}, u32[]{:S(2)}) copy-start(bf16[4,256,1024]{2,1,0:T(8,128)(2,1)} %get-tuple-element.24.x_ref) | copy-start | bytes 6291460
  149.6 2.8 %copy-start.8 = (bf16[2,1024,1024]{2,1,0:T(8,128)(2,1)S(1)}, bf16[2,1024,1024]{2,1,0:T(8,128)(2,1)}, u32[]{:S(2)}) copy-start(bf16[2,1024,1024]{2,1,0:T(8,128)(2,1)} %param.10) | copy-start | bytes 12582916

commit v4 on v3

--- a/solution.py
+++ b/solution.py
@@ -86,13 +86,13 @@
     current = frames
     flag_f = cloud_mask.astype(jnp.float32)[:, :, None]
     for layer in range(STACK_LEVELS):
+        chunks = kv_chunks(current, norm_gain[layer][None, :], flag_f, qkv_weight, layer, n_dev)
+        pieces = lax.all_to_all(chunks, everyone, 0, 0, tiled=True)
+        chunks, current = lax.optimization_barrier((chunks, current))
         xf = current.astype(jnp.float32)
         in_msq = jnp.mean(xf * xf, -1, keepdims=True) + 1e-05
         normalized_output = (xf * lax.rsqrt(in_msq) * norm_gain[layer]).astype(jnp.bfloat16)
         flat = normalized_output.reshape(-1, width)
-        pieces = lax.all_to_all(
-            kv_chunks(current, norm_gain[layer][None, :], flag_f, qkv_weight, layer, n_dev), everyone, 0, 0, tiled=True
-        )
         rows = pieces.shape[1]
         kv = pieces.reshape(n_date, n_space, rows, dates_here * HEAD).sum(1)
         kv = lax.optimization_barrier(kv).reshape(n_date, rows, dates_here, HEAD)

time: 157 us -> 162 us (1.032)
  waiting for transfers between devices: 36.7 us -> 30.6 us
  matrix products: 21.4 us -> 26.3 us
  starting transfers between devices: 37.9 us -> 41.9 us
  local copies, waits for them, and re-layouts: 29.8 us -> 32.2 us
    all_to_all x2, waiting for transfers between devices: 9.68 us -> 3.64 us  [shards(): pieces = lax.all_to_all(chunks, everyone, 0, 0, tiled=True)]
    all_to_all x2, starting transfers between devices: 12.1 us -> 16 us  [shards(): back = lax.all_to_all(outgoing, everyone, 0, 0, tiled=True)]
    dot_general x2, matrix products: 1.82 us -> 4.99 us  [shards(): jnp.einsum('tshe,thef->tshf', query, state_b, preferred_element_type=jnp....]
    reshape x2, local copies, waits for them, and re-layouts: 6.67 us -> 9.01 us  [shards(): query = feature(proj_q).astype(jnp.bfloat16).reshape(dates_here, tokens_h...]
    dot_general x2, matrix products: 11.4 us -> 13.4 us  [shards(): jnp.dot(flat, qkv_weight[layer, :, :width], preferred_element_type=jnp.fl...]
    unnamed x20 -> x16, local copies, waits for them, and re-layouts: 5.43 us -> 4.16 us
  transfers between devices with their start and end apart: 5 -> 5, of which waited for: 4 -> 4; matrix products, arithmetic and copies ran while one was open for 22% -> 25% of each run, Pallas kernels for 7% -> 7%
where the time goes in v4:
time: 162 us; the launch traced here: 161 us
  starting transfers between devices  41.9 us (26%)
  local copies, waits for them, and re-layouts  32.2 us (20%)
  waiting for transfers between devices  30.6 us (19%)
  matrix products  26.3 us (16%)
  Pallas kernels  22 us (14%)
  other arithmetic  7.52 us (5%)
    all_to_all x2, waiting for transfers between devices, shards(): back = lax.all_to_all(outgoing, everyone, 0, 0, tiled=True)  26.9 us
    pallas_call x2, Pallas kernels, kv_chunks(): pl.pallas_call(body, grid=(dates,), out_shape=jax.ShapeDtypeStruct((n_dev...  22 us
    all_to_all x2, starting transfers between devices, shards(): back = lax.all_to_all(outgoing, everyone, 0, 0, tiled=True)  16 us
    all_to_all x2, starting transfers between devices, shards(): pieces = lax.all_to_all(chunks, everyone, 0, 0, tiled=True)  14.3 us
    dot_general x2, matrix products, shards(): jnp.dot(flat, qkv_weight[layer, :, :width], preferred_element_type=jnp.fl...  13.4 us
    all_to_all x1, starting transfers between devices, shards(): from_each = lax.all_to_all(to_each, everyone, 0, 0, tiled=True)  11.5 us
    reshape x2, local copies, waits for them, and re-layouts, shards(): query = feature(proj_q).astype(jnp.bfloat16).reshape(dates_here, tokens_h...  9.01 us
    convert_element_type x2, local copies, waits for them, and re-layouts, shards(): query = feature(proj_q).astype(jnp.bfloat16).reshape(dates_here, tokens_h...  7.88 us
  transfers between devices with their start and end apart: 5, of which 4 were waited for; matrix products, arithmetic and copies ran while one was open for 25% of the time, Pallas kernels for 7%

profile of v4, /device:TPU:1, one launch (start us, length us, event | category | flops | bytes accessed | tf_op | source)
XLA Modules:
  0.0 160.6 jit_solution(13674200925680640164)
XLA Ops:
  1.4 11.5 %all-to-all-start = ((f32[128,2,4]{2,1,0:T(2,128)}), f32[128,2,4]{2,1,0:T(2,128)S(1)}, u32[]{:S(2)}, u32[]{:S(2)}) async-start(f32[128,2,4]{2,1,0:T(2,128)} %bitcast.2), calls=%async_computation | async-start | bytes 262144 | tf_op jit(solution)/shard_map/all_to_all | solution.py:82
  12.9 1.4 fusion.54
  15.0 1.0 copy.63.m_ref
  16.0 11.0 %shard_map.73 = f32[128,8,256]{2,1,0:T(8,128)} custom-call(bf16[4,256,1024]{2,1,0:T(8,128)(2,1)} %x_ref.1, f32[1,1024]{1,0:T(1,128)} %get-tuple-element.22.g_ref, f32[4,256,1]{2,1,0:T(8,128)} %copy.63.m_ref, bf16[2,1024,3072]{2,1,0:T(8,128)(2,1)} %wv_ref.3, bf16[2,1024,3072]{2,1,0:T(8,128)(2,1)} %wv_ref.3), custom_call_target="tpu_custom_call" | custom-call | tf_op jit(solution)/shard_map/pallas_call | solution.py:54
  27.5 1.9 %fusion.2 = bf16[4,256,1024]{2,1,0:T(8,128)(2,1)} fusion(bf16[4,256,1024]{2,1,0:T(8,128)(2,1)S(1)} %copy-done, f32[1024]{0:T(1024)S(1)} %bitcast.90, f32[4,256]{1,0:T(4,128)S(1)} %add_rsqrt_fusion.3), kind=kLoop, calls=%fused_computation.12 | loop fusion | flops 4194304 | bytes 4202496 | tf_op jit(solution)/shard_map/convert_element_type | solution.py:94
  29.4 9.8 %all-to-all-start.1 = ((f32[128,8,256]{2,1,0:T(8,128)}), f32[128,8,256]{2,1,0:T(8,128)S(1)}, u32[]{:S(2)}, u32[]{:S(2)}) async-start(f32[128,8,256]{2,1,0:T(8,128)} %shard_map.73), calls=%async_computation.1 | async-start | bytes 2097152 | tf_op jit(solution)/shard_map/all_to_all | solution.py:90
  39.2 7.0 %fusion.10 = bf16[1024,1024]{1,0:T(8,128)(2,1)} fusion(bf16[1024,1024]{1,0:T(8,128)(2,1)} %bitcast.80, bf16[2,1024,3072]{2,1,0:T(8,128)(2,1)} %wv_ref.3), kind=kOutput, calls=%fused_computation.20 | convolution fusion | flops 2152726528 | bytes 6291456 | tf_op jit(solution)/shard_map/dot_general | solution.py:105
  46.2 3.9 %copy.68 = bf16[1024,1024]{0,1:T(8,128)(2,1)} copy(bf16[1024,1024]{1,0:T(8,128)(2,1)} %fusion.10) | data formatting | bytes 4194304 | tf_op jit(solution)/shard_map/convert_element_type | solution.py:108
  50.1 4.5 %reshape.166 = bf16[4,256,16,64]{1,0,3,2:T(4,128)(2,1)} reshape(bf16[1024,1024]{0,1:T(8,128)(2,1)} %copy.68) | data formatting | bytes 4194304 | tf_op jit(solution)/shard_map/reshape | solution.py:109
  55.1 2.2 %fusion.21 = (f32[64,64]{1,0:T(8,128)S(1)}, f32[64,64]{1,0:T(8,128)S(1)}) fusion(f32[64]{0:T(128)S(1)} %broadcast_in_dim.75, pred[64,64]{1,0:T(8,128)(4,1)S(1)} %get-tuple-element.30, pred[64,64]{1,0:T(8,128)(4,1)S(1)} %get-tuple-element.29, f32[64]{0:T(128)S(1)} %broadcast_in_dim.69), kind=kLoop, calls=%fused_computation.37 | loop fusion | flops 1302528 | bytes 41472 | tf_op jit(solution)/shard_map/reduce_prod | solution.py:102
  58.6 0.9 broadcast_in_dim.74
  59.5 9.2 %all-to-all-start.2 = ((bf16[128,4,512]{2,1,0:T(4,128)(2,1)}), bf16[128,4,512]{2,1,0:T(4,128)(2,1)S(1)}, u32[]{:S(2)}, u32[]{:S(2)}) async-start(bf16[128,4,512]{2,1,0:T(4,128)(2,1)} %bitcast.10), calls=%async_computation.2 | async-start | bytes 1048576 | tf_op jit(solution)/shard_map/all_to_all | solution.py:116
  68.8 13.4 %all-to-all-done.2 = bf16[128,4,512]{2,1,0:T(4,128)(2,1)S(1)} async-done(((bf16[128,4,512]{2,1,0:T(4,128)(2,1)}), bf16[128,4,512]{2,1,0:T(4,128)(2,1)S(1)}, u32[]{:S(2)}, u32[]{:S(2)}) %all-to-all-start.2) | async-done | bytes 524320 | tf_op jit(solution)/shard_map/all_to_all | solution.py:116
  82.3 0.9 copy.69
  83.2 1.6 %reshape.168 = bf16[4,16,64,64]{3,2,1,0:T(8,128)(2,1)S(1)} reshape(bf16[4,128,512]{2,1,0:T(8,128)(2,1)} %copy.69) | data formatting | bytes 1048576 | tf_op jit(solution)/shard_map/reshape | solution.py:117
  84.8 2.5 %fusion.17 = (f32[4,256,16]{1,2,0:T(8,128)S(1)}, f32[4,16,64,256]{3,2,1,0:T(8,128)S(1)}) fusion(bf16[4,16,64,64]{3,2,1,0:T(8,128)(2,1)S(1)} %reshape.168, bf16[4,256,16,64]{1,0,3,2:T(4,128)(2,1)} %reshape.166), kind=kOutput, calls=%fused_computation.31 | convolution fusion | flops 136298496 | bytes 6881280 | tf_op jit(solution)/shard_map/tshe,thef->tshf/dot_general | solution.py:119
  87.9 1.6 %copy-done.5 = bf16[2,1024,1024]{2,1,0:T(8,128)(2,1)S(1)} copy-done((bf16[2,1024,1024]{2,1,0:T(8,128)(2,1)S(1)}, bf16[2,1024,1024]{2,1,0:T(8,128)(2,1)}, u32[]{:S(2)}) %copy-start.5) | copy-done | bytes 4194328
  89.5 3.7 %fusion.3.x_ref = bf16[4,256,1024]{2,1,0:T(8,128)(2,1)} fusion(bf16[4,256,1024]{2,1,0:T(8,128)(2,1)S(1)} %copy-done, bf16[4,256,1024]{1,2,0:T(8,128)(2,1)S(1)} %bitcast.82, bf16[2,1024,1024]{2,1,0:T(8,128)(2,1)S(1)} %copy-done.5), kind=kOutput, calls=%fused_computation.13 | convolution fusion | flops 2150629376 | bytes 8388608 | tf_op jit(solution)/shard_map/dot_general | solution.py:125
  93.2 11.0 %shard_map.74 = f32[128,8,256]{2,1,0:T(8,128)} custom-call(bf16[4,256,1024]{2,1,0:T(8,128)(2,1)} %fusion.3.x_ref, f32[1,1024]{1,0:T(1,128)} %get-tuple-element.21.g_ref, f32[4,256,1]{2,1,0:T(8,128)} %copy.63.m_ref, bf16[2,1024,3072]{2,1,0:T(8,128)(2,1)} %wv_ref.3, bf16[2,1024,3072]{2,1,0:T(8,128)(2,1)} %wv_ref.3), custom_call_target="tpu_custom_call" | custom-call | tf_op jit(solution)/shard_map/pallas_call | solution.py:54
  104.2 4.6 %all-to-all-start.3 = ((f32[128,8,256]{2,1,0:T(8,128)}), f32[128,8,256]{2,1,0:T(8,128)S(1)}, u32[]{:S(2)}, u32[]{:S(2)}) async-start(f32[128,8,256]{2,1,0:T(8,128)} %shard_map.74), calls=%async_computation.3 | async-start | bytes 2097152 | tf_op jit(solution)/shard_map/all_to_all | solution.py:90
  109.8 6.4 %fusion.13 = bf16[1024,1024]{1,0:T(8,128)(2,1)} fusion(bf16[1024,1024]{1,0:T(8,128)(2,1)S(1)} %bitcast.83, bf16[2,1024,3072]{2,1,0:T(8,128)(2,1)} %wv_ref.3), kind=kOutput, calls=%fused_computation.23 | convolution fusion | flops 2152726528 | bytes 6291456 | tf_op jit(solution)/shard_map/dot_general | solution.py:105
  116.2 4.0 %copy.76 = bf16[1024,1024]{0,1:T(8,128)(2,1)} copy(bf16[1024,1024]{1,0:T(8,128)(2,1)} %fusion.13) | data formatting | bytes 4194304 | tf_op jit(solution)/shard_map/convert_element_type | solution.py:108
  120.2 4.5 %reshape.173 = bf16[4,256,16,64]{1,0,3,2:T(4,128)(2,1)} reshape(bf16[1024,1024]{0,1:T(8,128)(2,1)} %copy.76) | data formatting | bytes 4194304 | tf_op jit(solution)/shard_map/reshape | solution.py:109
  124.6 3.0 %all-to-all-done.3 = f32[128,8,256]{2,1,0:T(8,128)S(1)} async-done(((f32[128,8,256]{2,1,0:T(8,128)}), f32[128,8,256]{2,1,0:T(8,128)S(1)}, u32[]{:S(2)}, u32[]{:S(2)}) %all-to-all-start.3) | async-done | bytes 1048608 | tf_op jit(solution)/shard_map/all_to_all | solution.py:90
  128.3 0.9 broadcast_in_dim.78
  129.3 6.9 %all-to-all-start.4 = ((bf16[128,4,512]{2,1,0:T(4,128)(2,1)}), bf16[128,4,512]{2,1,0:T(4,128)(2,1)S(1)}, u32[]{:S(2)}, u32[]{:S(2)}) async-start(bf16[128,4,512]{2,1,0:T(4,128)(2,1)} %bitcast.21), calls=%async_computation.4 | async-start | bytes 1048576 | tf_op jit(solution)/shard_map/all_to_all | solution.py:116
  136.2 13.5 %all-to-all-done.4 = bf16[128,4,512]{2,1,0:T(4,128)(2,1)S(1)} async-done(((bf16[128,4,512]{2,1,0:T(4,128)(2,1)}), bf16[128,4,512]{2,1,0:T(4,128)(2,1)S(1)}, u32[]{:S(2)}, u32[]{:S(2)}) %all-to-all-start.4) | async-done | bytes 524320 | tf_op jit(solution)/shard_map/all_to_all | solution.py:116
  149.7 0.9 copy.77
  150.6 1.6 %reshape.175 = bf16[4,16,64,64]{3,2,1,0:T(8,128)(2,1)S(1)} reshape(bf16[4,128,512]{2,1,0:T(8,128)(2,1)} %copy.77) | data formatting | bytes 1048576 | tf_op jit(solution)/shard_map/reshape | solution.py:117
  152.2 2.5 %fusion.14 = (f32[4,256,16]{1,2,0:T(8,128)S(1)}, f32[4,16,64,256]{3,2,1,0:T(8,128)S(1)}) fusion(bf16[4,16,64,64]{3,2,1,0:T(8,128)(2,1)S(1)} %reshape.175, bf16[4,256,16,64]{1,0,3,2:T(4,128)(2,1)} %reshape.173), kind=kOutput, calls=%fused_computation.26 | convolution fusion | flops 136298496 | bytes 6881280 | tf_op jit(solution)/shard_map/tshe,thef->tshf/dot_general | solution.py:119
  155.3 1.6 %copy-done.6 = bf16[2,1024,1024]{2,1,0:T(8,128)(2,1)S(1)} copy-done((bf16[2,1024,1024]{2,1,0:T(8,128)(2,1)S(1)}, bf16[2,1024,1024]{2,1,0:T(8,128)(2,1)}, u32[]{:S(2)}) %copy-start.6) | copy-done | bytes 4194328
  156.9 3.7 %fusion.7 = bf16[4,256,1024]{2,1,0:T(8,128)(2,1)} fusion(bf16[4,256,1024]{2,1,0:T(8,128)(2,1)S(1)} %copy-done.1, bf16[4,256,1024]{1,2,0:T(8,128)(2,1)S(1)} %bitcast.81, bf16[2,1024,1024]{2,1,0:T(8,128)(2,1)S(1)} %copy-done.6), kind=kOutput, calls=%fused_computation.17 | convolution fusion | flops 2150629376 | bytes 8388608 | tf_op jit(solution)/shard_map/dot_general | solution.py:125
  (49 shorter events, 7.2 us)
Async XLA Ops:
  1.4 27.9 %all-to-all-start = ((f32[128,2,4]{2,1,0:T(2,128)}), f32[128,2,4]{2,1,0:T(2,128)S(1)}, u32[]{:S(2)}, u32[]{:S(2)}) async-start(f32[128,2,4]{2,1,0:T(2,128)} %bitcast.2), calls=%async_computation | async-start | bytes 262144 | tf_op jit(solution)/shard_map/all_to_all | solution.py:82
  16.0 11.0 %copy-start = (bf16[4,256,1024]{2,1,0:T(8,128)(2,1)S(1)}, bf16[4,256,1024]{2,1,0:T(8,128)(2,1)}, u32[]{:S(2)}) copy-start(bf16[4,256,1024]{2,1,0:T(8,128)(2,1)} %x_ref.1) | copy-start | bytes 6291460
  16.0 11.5 %copy-start.3 = (f32[1,1024]{1,0:T(1,128)S(1)}, f32[1,1024]{1,0:T(1,128)}, u32[]{:S(2)}) copy-start(f32[1,1024]{1,0:T(1,128)} %get-tuple-element.22.g_ref) | copy-start | bytes 12292
  29.4 28.6 %all-to-all-start.1 = ((f32[128,8,256]{2,1,0:T(8,128)}), f32[128,8,256]{2,1,0:T(8,128)S(1)}, u32[]{:S(2)}, u32[]{:S(2)}) async-start(f32[128,8,256]{2,1,0:T(8,128)} %shard_map.73), calls=%async_computation.1 | async-start | bytes 2097152 | tf_op jit(solution)/shard_map/all_to_all | solution.py:90
  50.1 18.6 %copy-start.4 = (f32[2,1024]{1,0:T(2,128)S(1)}, f32[2,1024]{1,0:T(2,128)}, u32[]{:S(2)}) copy-start(f32[2,1024]{1,0:T(2,128)} %param.12) | copy-start | bytes 24580
  59.5 22.7 %all-to-all-start.2 = ((bf16[128,4,512]{2,1,0:T(4,128)(2,1)}), bf16[128,4,512]{2,1,0:T(4,128)(2,1)S(1)}, u32[]{:S(2)}, u32[]{:S(2)}) async-start(bf16[128,4,512]{2,1,0:T(4,128)(2,1)} %bitcast.10), calls=%async_computation.2 | async-start | bytes 1048576 | tf_op jit(solution)/shard_map/all_to_all | solution.py:116
  87.3 2.2 %copy-start.5 = (bf16[2,1024,1024]{2,1,0:T(8,128)(2,1)S(1)}, bf16[2,1024,1024]{2,1,0:T(8,128)(2,1)}, u32[]{:S(2)}) copy-start(bf16[2,1024,1024]{2,1,0:T(8,128)(2,1)} %param.10) | copy-start | bytes 12582916
  93.2 15.6 %copy-start.1 = (bf16[4,256,1024]{2,1,0:T(8,128)(2,1)S(1)}, bf16[4,256,1024]{2,1,0:T(8,128)(2,1)}, u32[]{:S(2)}) copy-start(bf16[4,256,1024]{2,1,0:T(8,128)(2,1)} %fusion.3.x_ref) | copy-start | bytes 6291460
  104.2 5.1 %copy-start.2 = (f32[1,1024]{1,0:T(1,128)S(1)}, f32[1,1024]{1,0:T(1,128)}, u32[]{:S(2)}) copy-start(f32[1,1024]{1,0:T(1,128)} %get-tuple-element.21.g_ref) | copy-start | bytes 12292
  104.2 23.5 %all-to-all-start.3 = ((f32[128,8,256]{2,1,0:T(8,128)}), f32[128,8,256]{2,1,0:T(8,128)S(1)}, u32[]{:S(2)}, u32[]{:S(2)}) async-start(f32[128,8,256]{2,1,0:T(8,128)} %shard_map.74), calls=%async_computation.3 | async-start | bytes 2097152 | tf_op jit(solution)/shard_map/all_to_all | solution.py:90
  129.3 20.4 %all-to-all-start.4 = ((bf16[128,4,512]{2,1,0:T(4,128)(2,1)}), bf16[128,4,512]{2,1,0:T(4,128)(2,1)S(1)}, u32[]{:S(2)}, u32[]{:S(2)}) async-start(bf16[128,4,512]{2,1,0:T(4,128)(2,1)} %bitcast.21), calls=%async_computation.4 | async-start | bytes 1048576 | tf_op jit(solution)/shard_map/all_to_all | solution.py:116
  154.7 2.2 %copy-start.6 = (bf16[2,1024,1024]{2,1,0:T(8,128)(2,1)S(1)}, bf16[2,1024,1024]{2,1,0:T(8,128)(2,1)}, u32[]{:S(2)}) copy-start(bf16[2,1024,1024]{2,1,0:T(8,128)(2,1)} %param.10) | copy-start | bytes 12582916
